TPU v7x, 512 devices: a whole 4x4x16 slice. The times are simulated.
512 devices in a mesh: mem: 16 (over z_hi, y, core), gx: 32 (over x, z_lo).
Axes of the slice: x: 4, y: 4, z: 16 (z_hi: 2, z_lo: 8; z = z_hi * 8 + z_lo), core: 2. Of those that a mesh axis runs over, the one named last changes fastest.
Arguments:
- weights: bfloat16 [16, 512, 32768], P('mem', 'gx'), may hold values from -6 to 6
- perturbations: bfloat16 [2, 16, 512, 32768], P(None, 'mem', 'gx'), may hold values from -3 to 3
- obs_cell: int32 [131072], P('gx'), may hold values from 0 to 524287
- obs_slot: int32 [131072], P('gx'), may hold values from 0 to 1
- innovation: float32 [131072], P('gx'), may hold values from -24 to 24
- obs_weight: float32 [131072], P('gx'), may hold values from 0.5 to 4
- obs_count: int32 [32], P('gx'), may hold values from 2048 to 4096, as said below
Outputs:
- gradient: float32 [16, 512, 32768], P('mem', 'gx')
Inputs may be any that keep to these rules, and one draw needn't show every extreme that they name: Slab s uses its first obs_count[s] observation slots, o = s * 4096 .. s * 4096 + obs_count[s] - 1; some slab is full and another holds 2048. `obs_cell`: the cell is numbered (x within the slab) * 512 * 64 + y * 64 + z; several observations may share a cell.
All inputs are finite; a program needn't handle non-finite values.
Results may differ from a plain program's by a relative error of at most 0.0029.
Values may be sent and summed in bfloat16 or wider, within the bound.
No kernel may reach another device: no remote copies, remote signals or barrier semaphores. Data moves between devices by JAX's collectives and lax.ppermute only.
A program may use at most 64 MiB of HBM per device.

v0:
```python
import jax
import jax.numpy as jnp
from jax import lax
from jax.sharding import PartitionSpec as P

NY = 512
NZ = 64


tap_reach = 15
corr_scale = 7.0


def padded_2(block, sides, width):
    for axis, dim in sides:
        count = lax.axis_size(axis)
        forward = [(i, i + 1) for i in range(count - 1)]
        backward = [(target, source) for source, target in forward]
        low = lax.ppermute(
            lax.slice_in_dim(block, block.shape[dim] - width, None, axis=dim), axis, forward
        )
        high = lax.ppermute(lax.slice_in_dim(block, 0, width, axis=dim), axis, backward)
        block = jnp.concatenate([low, block, high], axis=dim)
    return block


def tap_values():
    offsets = jnp.arange(-tap_reach, tap_reach + 1).astype(jnp.float32)
    bell = jnp.exp(-offsets * offsets / (2.0 * corr_scale * corr_scale))
    return (bell / jnp.sqrt(jnp.sum(bell * bell))).astype(jnp.bfloat16)


def band_matrix(count_out, count_in, start):
    out_pos = jnp.arange(count_out)
    in_pos = jnp.arange(count_in)
    offsets = in_pos[None, :] - out_pos[:, None] - start
    tap_table = tap_values()
    lookup = tap_table[jnp.clip(offsets + tap_reach, 0, 2 * tap_reach)]
    return jnp.where(jnp.abs(offsets) <= tap_reach, lookup, jnp.zeros_like(lookup))


def along_z(field):
    members, slab_rows, plane_cells = field.shape
    band_z = band_matrix(NZ, NZ, 0)
    grid = field.reshape(members, slab_rows, NY, NZ)
    result = jnp.einsum("mxyq,zq->mxyz", grid, band_z, preferred_element_type=jnp.float32)
    return result.reshape(members, slab_rows, plane_cells)


def along_y(field):
    members, slab_rows, plane_cells = field.shape
    band_y = band_matrix(NY, NY, 0)
    grid = field.reshape(members, slab_rows, NY, NZ)
    result = jnp.einsum("mxqz,yq->mxyz", grid, band_y, preferred_element_type=jnp.float32)
    return result.reshape(members, slab_rows, plane_cells)


def along_x(padded, slab_rows):
    band_x = band_matrix(slab_rows, slab_rows + 2 * tap_reach, tap_reach)
    return jnp.einsum("ip,mpc->mic", band_x, padded, preferred_element_type=jnp.float32)


def local(weights, perturbations, obs_cell, obs_slot, innovation, obs_weight, obs_count):
    members, slab_rows, plane_cells = weights.shape
    slot_count = perturbations.shape[0]
    z_smooth = along_z(weights).astype(jnp.bfloat16)
    y_smooth = along_y(z_smooth).astype(jnp.bfloat16)
    padded = padded_2(y_smooth, (("gx", 1),), tap_reach)
    smoothed = along_x(padded, slab_rows)
    partial_sum = jnp.sum(perturbations.astype(jnp.float32) * smoothed[None], axis=1)
    increment = lax.psum(partial_sum, "mem")
    flat_increment = increment.reshape(slot_count, slab_rows * plane_cells)
    sampled = flat_increment[obs_slot, obs_cell]
    live_mask = (jnp.arange(obs_cell.shape[0]) < obs_count[0]).astype(jnp.float32)
    residual = live_mask * obs_weight * (sampled - innovation)
    forcing = (
        jnp.zeros((slot_count, slab_rows * plane_cells), jnp.float32)
        .at[obs_slot, obs_cell]
        .add(residual)
    )
    forcing = forcing.reshape(slot_count, 1, slab_rows, plane_cells)
    adjoint_source = jnp.sum(perturbations.astype(jnp.float32) * forcing, axis=0).astype(
        jnp.bfloat16
    )
    padded_back = padded_2(adjoint_source, (("gx", 1),), tap_reach)
    x_back = along_x(padded_back, slab_rows).astype(jnp.bfloat16)
    y_back = along_y(x_back).astype(jnp.bfloat16)
    return weights.astype(jnp.float32) + along_z(y_back)


def solution(mesh):
    return jax.shard_map(
        local,
        mesh=mesh,
        in_specs=(
            P("mem", "gx", None),
            P(None, "mem", "gx", None),
            P("gx"),
            P("gx"),
            P("gx"),
            P("gx"),
            P("gx"),
        ),
        out_specs=P("mem", "gx", None),
        check_vma=False,
    )
```

profile of v0, /device:TPU:29, one launch (start us, length us, event | category | flops | bytes accessed | tf_op | source)
XLA Modules:
  0.0 598.7 jit_solution(7883785329792114746)
XLA Ops:
  6.5 0.0 all-reduce.2.cloned.1.call-start
  6.5 0.6 multiply_reduce_fusion.1
  7.9 0.7 fusion.197
  8.6 0.7 fusion.198
  9.3 0.1 reshape.224
  9.4 24.4 %gather_fusion = bf16[4096]{0:T(1024)(128)(2,1)S(1)} fusion(bf16[31]{0:T(256)(128)(2,1)S(1)} %divide_convert_fusion, s32[4096]{0:T(1024)S(1)} %broadcast_clamp_fusion), kind=kCustom, calls=%fused_computation | custom fusion | bytes 32768 | tf_op jit(solution)/shard_map/gather | solution.py:38
  33.8 0.1 reshape.223
  33.9 0.0 copy-done.1
  33.9 2.3 reshape.170
  36.2 0.8 convolution_convert_fusion.1
  37.1 22.6 %fusion.104 = f32[512,1024]{0,1:S(1)} fusion(bf16[512,1024]{0,1:T(8,128)(2,1)S(1)} %bitcast.898, bf16[]{:T(256)} %bitcast.48, bf16[]{:T(256)} %bitcast.49, bf16[]{:T(256)} %bitcast.50, bf16[]{:T(256)} %bitcast.51, bf16[]{:T(256)} %bitcast.52, bf16[]{:T(256)} %bitcast.54, bf16[]{:T(256)} %bitcast.53, bf16[]{:T(256)} %bitcast.1, bf16[]{:T(256)} %bitcast.3, ...), kind=kOutput, calls=%fused_computation.119 | convolution fusion | flops 555220992 | bytes 3145790
  59.6 0.1 convert_bitcast_fusion.1
  59.8 1.1 copy.9
  60.9 1.7 convert_element_type.100
  62.6 1.5 fusion.196
  64.1 3.5 collective-permute-start
  67.7 11.4 %collective-permute-start.1 = (bf16[1,15,32768]{2,1,0:T(8,128)(2,1)}, bf16[1,15,32768]{2,1,0:T(8,128)(2,1)}, u32[]{:S(2)}, u32[]{:S(2)}) collective-permute-start(bf16[1,15,32768]{2,1,0:T(8,128)(2,1)} %get-tuple-element.8), channel_id=1, source_target_pairs={{1,0},{2,1},{3,2},{4,3},{5,4},{6,5},{7,6},{8,7},{9,8},{10,9},{11,1... | collective-permute-start | bytes 2949128 | tf_op jit(solution)/shard_map/ppermute | solution.py:22
  79.1 0.1 reshape.232
  79.2 4.8 gather_fusion.1
  84.0 0.1 reshape.231
  84.1 0.0 copy-start
  84.1 16.1 %collective-permute-done = bf16[1,15,32768]{2,1,0:T(8,128)(2,1)} collective-permute-done((bf16[1,15,32768]{2,1,0:T(8,128)(2,1)}, bf16[1,15,32768]{2,1,0:T(8,128)(2,1)}, u32[]{:S(2)}, u32[]{:S(2)}) %collective-permute-start) | collective-permute-done | bytes 983072 | tf_op jit(solution)/shard_map/ppermute | solution.py:19
  100.2 16.3 %collective-permute-done.1 = bf16[1,15,32768]{2,1,0:T(8,128)(2,1)} collective-permute-done((bf16[1,15,32768]{2,1,0:T(8,128)(2,1)}, bf16[1,15,32768]{2,1,0:T(8,128)(2,1)}, u32[]{:S(2)}, u32[]{:S(2)}) %collective-permute-start.1) | collective-permute-done | bytes 983072 | tf_op jit(solution)/shard_map/ppermute | solution.py:22
  116.5 2.5 convolution_bitcast_fusion
  119.0 0.0 copy-done
  119.0 0.3 fusion.1
  119.4 5.2 copy.13
  124.6 0.0 all-reduce.2.cloned.1.call-update
  125.3 0.0 copy-done.4
  125.3 0.1 multiply_reduce_fusion
  125.5 0.1 and_reduce_fusion
  125.7 298.1 %all-reduce.2.cloned.1.call-done = f32[2,524288]{1,0:T(2,128)} async-done(((f32[2,524288]{1,0:T(2,128)}), f32[2,524288]{1,0:T(2,128)}) %all-reduce.2.cloned.1.call-update) | async-done | bytes 4194320 | tf_op jit(solution)/shard_map/psum | solution.py:71
  423.8 50.2 %gather_fusion.2 = f32[4096]{0:T(1024)S(1)} fusion(f32[2,524288]{1,0:T(2,128)} %all-reduce.2.cloned.1.call-done, s32[4096]{0:T(1024)S(1)} %bitcast.891), kind=kCustom, calls=%fused_computation.2 | custom fusion | bytes 65536 | tf_op jit(solution)/shard_map/gather | solution.py:73
  474.1 24.1 %scatter_custom_fusion = f32[1048576]{0:T(1024)} fusion(s32[4096]{0:T(1024)S(1)} %broadcast_select_fusion, f32[4096]{0:T(1024)S(1)} %subtract_multiply_fusion, f32[]{:T(128)} %constant.13.clone.1), kind=kCustom, calls=%fused_computation.22 | custom fusion | flops 4096 | bytes 4194308
  498.1 5.0 reshape.173
  503.1 2.8 fusion.2
  505.9 0.2 fusion.195
  506.1 3.3 collective-permute-start.2
  509.4 11.3 %collective-permute-start.3 = (bf16[1,15,32768]{2,1,0:T(8,128)(2,1)S(1)}, bf16[1,15,32768]{2,1,0:T(8,128)(2,1)S(1)}, u32[]{:S(2)}, u32[]{:S(2)}) collective-permute-start(bf16[1,15,32768]{2,1,0:T(8,128)(2,1)S(1)} %get-tuple-element.6), channel_id=1, source_target_pairs={{1,0},{2,1},{3,2},{4,3},{5,4},{6,5},{7,6},{8,7},{9,8},{10,9},{11,1... | collective-permute-start | bytes 2949128 | tf_op jit(solution)/shard_map/ppermute | solution.py:22
  520.8 21.3 %collective-permute-done.2 = bf16[1,15,32768]{2,1,0:T(8,128)(2,1)S(1)} collective-permute-done((bf16[1,15,32768]{2,1,0:T(8,128)(2,1)S(1)}, bf16[1,15,32768]{2,1,0:T(8,128)(2,1)S(1)}, u32[]{:S(2)}, u32[]{:S(2)}) %collective-permute-start.2) | collective-permute-done | bytes 983072 | tf_op jit(solution)/shard_map/ppermute | solution.py:19
  542.1 15.8 %collective-permute-done.3 = bf16[1,15,32768]{2,1,0:T(8,128)(2,1)S(1)} collective-permute-done((bf16[1,15,32768]{2,1,0:T(8,128)(2,1)S(1)}, bf16[1,15,32768]{2,1,0:T(8,128)(2,1)S(1)}, u32[]{:S(2)}, u32[]{:S(2)}) %collective-permute-start.3) | collective-permute-done | bytes 983072 | tf_op jit(solution)/shard_map/ppermute | solution.py:22
  557.9 1.0 fusion
  558.9 2.3 reshape.175
  561.2 0.8 copy.10
  562.0 22.6 %fusion.102 = f32[512,1024]{0,1:S(1)} fusion(bf16[512,1024]{0,1:T(8,128)(2,1)S(1)} %bitcast.897, bf16[]{:T(256)} %bitcast.48, bf16[]{:T(256)} %bitcast.49, bf16[]{:T(256)} %bitcast.50, bf16[]{:T(256)} %bitcast.51, bf16[]{:T(256)} %bitcast.52, bf16[]{:T(256)} %bitcast.54, bf16[]{:T(256)} %bitcast.53, bf16[]{:T(256)} %bitcast.1, bf16[]{:T(256)} %bitcast.3, ...), kind=kOutput, calls=%fused_computation.118 | convolution fusion | flops 555220992 | bytes 3145790
  584.6 2.7 fusion.13
  587.3 3.0 reshape.177
  590.3 1.5 convert_add_fusion
  (24 shorter events, 0.2 us)
Async XLA Ops:
  6.5 417.3 %all-reduce.2.cloned.1.call-start = ((), (), s32[]{:S(2)}) async-start(), calls=%async_computation | async-start | bytes 8388608 | tf_op jit(solution)/shard_map/psum | solution.py:71
  9.4 24.5 %copy-start.1 = (bf16[1,16,32768]{2,1,0:T(8,128)(2,1)S(1)}, bf16[1,16,32768]{2,1,0:T(8,128)(2,1)}, u32[]{:S(2)}) copy-start(bf16[1,16,32768]{2,1,0:T(8,128)(2,1)} %param.7) | copy-start | bytes 3145732
  64.1 36.1 %collective-permute-start = (bf16[1,15,32768]{2,1,0:T(8,128)(2,1)}, bf16[1,15,32768]{2,1,0:T(8,128)(2,1)}, u32[]{:S(2)}, u32[]{:S(2)}) collective-permute-start(bf16[1,15,32768]{2,1,0:T(8,128)(2,1)} %get-tuple-element.7), channel_id=1, source_target_pairs={{0,1},{1,2},{2,3},{3,4},{4,5},{5,6},{6,7},{7,8},{8,9},{9,10},{10,1... | collective-permute-start | bytes 2949128 | tf_op jit(solution)/shard_map/ppermute | solution.py:19
  67.7 48.8 %collective-permute-start.1 = (bf16[1,15,32768]{2,1,0:T(8,128)(2,1)}, bf16[1,15,32768]{2,1,0:T(8,128)(2,1)}, u32[]{:S(2)}, u32[]{:S(2)}) collective-permute-start(bf16[1,15,32768]{2,1,0:T(8,128)(2,1)} %get-tuple-element.8), channel_id=1, source_target_pairs={{1,0},{2,1},{3,2},{4,3},{5,4},{6,5},{7,6},{8,7},{9,8},{10,9},{11,1... | collective-permute-start | bytes 2949128 | tf_op jit(solution)/shard_map/ppermute | solution.py:22
  84.1 34.9 %copy-start = (bf16[2,1,16,32768]{3,2,1,0:T(8,128)(2,1)S(1)}, bf16[2,1,16,32768]{3,2,1,0:T(8,128)(2,1)}, u32[]{:S(2)}) copy-start(bf16[2,1,16,32768]{3,2,1,0:T(8,128)(2,1)} %param.8) | copy-start | bytes 6291460
  124.6 0.7 copy-start.3
  124.6 0.7 copy-start.4
  124.6 0.8 copy-start.7
  124.6 0.9 copy-start.8
  423.8 50.3 %copy-start.5 = (f32[4096]{0:T(1024)S(1)}, f32[4096]{0:T(1024)}, u32[]{:S(2)}) copy-start(f32[4096]{0:T(1024)} %param.11) | copy-start | bytes 49156
  423.8 50.3 %copy-start.6 = (f32[4096]{0:T(1024)S(1)}, f32[4096]{0:T(1024)}, u32[]{:S(2)}) copy-start(f32[4096]{0:T(1024)} %param.12) | copy-start | bytes 49156
  506.1 35.9 %collective-permute-start.2 = (bf16[1,15,32768]{2,1,0:T(8,128)(2,1)S(1)}, bf16[1,15,32768]{2,1,0:T(8,128)(2,1)S(1)}, u32[]{:S(2)}, u32[]{:S(2)}) collective-permute-start(bf16[1,15,32768]{2,1,0:T(8,128)(2,1)S(1)} %get-tuple-element.5), channel_id=1, source_target_pairs={{0,1},{1,2},{2,3},{3,4},{4,5},{5,6},{6,7},{7,8},{8,9},{9,10},{10,1... | collective-permute-start | bytes 2949128 | tf_op jit(solution)/shard_map/ppermute | solution.py:19
  509.4 48.4 %collective-permute-start.3 = (bf16[1,15,32768]{2,1,0:T(8,128)(2,1)S(1)}, bf16[1,15,32768]{2,1,0:T(8,128)(2,1)S(1)}, u32[]{:S(2)}, u32[]{:S(2)}) collective-permute-start(bf16[1,15,32768]{2,1,0:T(8,128)(2,1)S(1)} %get-tuple-element.6), channel_id=1, source_target_pairs={{1,0},{2,1},{3,2},{4,3},{5,4},{6,5},{7,6},{8,7},{9,8},{10,9},{11,1... | collective-permute-start | bytes 2949128 | tf_op jit(solution)/shard_map/ppermute | solution.py:22
  587.3 3.0 copy-start.2
Sparse Core Ops, SparseCore 0:
  124.7 299.0 all-reduce.1
where the time goes:
time: 601 us; the launch traced here: 599 us
  waiting for transfers between devices  368 us (61%)
  local copies, waits for them, and re-layouts  104 us (17%)
  matrix products  52.2 us (9%)
  other arithmetic  29.8 us (5%)
  starting transfers between devices  29.6 us (5%)
  between operations  15.1 us (3%)
    psum x1, waiting for transfers between devices, local(): increment = lax.psum(partial_sum, 'mem')  298 us
    gather x1, local copies, waits for them, and re-layouts, local(): sampled = flat_increment[obs_slot, obs_cell]  50.2 us
    unnamed x2, matrix products  45.1 us
    ppermute x2, waiting for transfers between devices, padded_2(): lax.ppermute(lax.slice_in_dim(block, block.shape[dim] - width, None, axis...  37.4 us
    ppermute x2, waiting for transfers between devices, padded_2(): lax.ppermute(lax.slice_in_dim(block, 0, width, axis=dim), axis, backward)  32.1 us
    gather x6, local copies, waits for them, and re-layouts, band_matrix(): lookup = tap_table[jnp.clip(offsets + tap_reach, 0, 2 * tap_reach)]  30.8 us
    unnamed x5, other arithmetic  24.6 us
    ppermute x2, starting transfers between devices, padded_2(): lax.ppermute(lax.slice_in_dim(block, 0, width, axis=dim), axis, backward)  22.8 us
  transfers between devices with their start and end apart: 5, of which 5 were waited for; matrix products, arithmetic and copies ran while one was open for 1% of the time, Pallas kernels for 0%

commit v1 on v0

--- a/solution.py
+++ b/solution.py
@@ -1,3 +1,4 @@
+import numpy as np
 import jax
 import jax.numpy as jnp
 from jax import lax
@@ -5,6 +6,7 @@
 
 NY = 512
 NZ = 64
+LANES = 128
 
 
 tap_reach = 15
@@ -25,18 +27,20 @@
 
 
 def tap_values():
-    offsets = jnp.arange(-tap_reach, tap_reach + 1).astype(jnp.float32)
-    bell = jnp.exp(-offsets * offsets / (2.0 * corr_scale * corr_scale))
-    return (bell / jnp.sqrt(jnp.sum(bell * bell))).astype(jnp.bfloat16)
+    offsets = np.arange(-tap_reach, tap_reach + 1).astype(np.float32)
+    bell = np.exp(-offsets * offsets / np.float32(2.0 * corr_scale * corr_scale)).astype(np.float32)
+    taps = (bell / np.sqrt(np.sum(bell * bell, dtype=np.float32))).astype(np.float32)
+    return taps.astype(jnp.bfloat16).astype(np.float32)
 
 
 def band_matrix(count_out, count_in, start):
-    out_pos = jnp.arange(count_out)
-    in_pos = jnp.arange(count_in)
+    out_pos = np.arange(count_out)
+    in_pos = np.arange(count_in)
     offsets = in_pos[None, :] - out_pos[:, None] - start
-    tap_table = tap_values()
-    lookup = tap_table[jnp.clip(offsets + tap_reach, 0, 2 * tap_reach)]
-    return jnp.where(jnp.abs(offsets) <= tap_reach, lookup, jnp.zeros_like(lookup))
+    taps = tap_values()
+    lookup = taps[np.clip(offsets + tap_reach, 0, 2 * tap_reach)]
+    band = np.where(np.abs(offsets) <= tap_reach, lookup, np.zeros_like(lookup))
+    return jnp.asarray(band.astype(jnp.bfloat16))
 
 
 def along_z(field):
@@ -63,25 +67,27 @@
 def local(weights, perturbations, obs_cell, obs_slot, innovation, obs_weight, obs_count):
     members, slab_rows, plane_cells = weights.shape
     slot_count = perturbations.shape[0]
+    nobs = obs_cell.shape[0]
+    rows = slab_rows * plane_cells // LANES
     z_smooth = along_z(weights).astype(jnp.bfloat16)
     y_smooth = along_y(z_smooth).astype(jnp.bfloat16)
     padded = padded_2(y_smooth, (("gx", 1),), tap_reach)
     smoothed = along_x(padded, slab_rows)
-    partial_sum = jnp.sum(perturbations.astype(jnp.float32) * smoothed[None], axis=1)
-    increment = lax.psum(partial_sum, "mem")
-    flat_increment = increment.reshape(slot_count, slab_rows * plane_cells)
-    sampled = flat_increment[obs_slot, obs_cell]
-    live_mask = (jnp.arange(obs_cell.shape[0]) < obs_count[0]).astype(jnp.float32)
+
+    obs_row = obs_cell // LANES
+    lane_hit = lax.broadcasted_iota(jnp.int32, (nobs, LANES), 1) == (obs_cell % LANES)[:, None]
+    s_rows = smoothed.reshape(rows, LANES)[obs_row]
+    s_val = jnp.sum(jnp.where(lane_hit, s_rows, 0.0), axis=1)
+    p_rows = perturbations.reshape(slot_count * rows, LANES)[obs_slot * rows + obs_row]
+    p_val = jnp.sum(jnp.where(lane_hit, p_rows.astype(jnp.float32), 0.0), axis=1)
+    sampled = lax.psum(p_val * s_val, "mem")
+
+    live_mask = (jnp.arange(nobs) < obs_count[0]).astype(jnp.float32)
     residual = live_mask * obs_weight * (sampled - innovation)
-    forcing = (
-        jnp.zeros((slot_count, slab_rows * plane_cells), jnp.float32)
-        .at[obs_slot, obs_cell]
-        .add(residual)
-    )
-    forcing = forcing.reshape(slot_count, 1, slab_rows, plane_cells)
-    adjoint_source = jnp.sum(perturbations.astype(jnp.float32) * forcing, axis=0).astype(
-        jnp.bfloat16
-    )
+    contrib = jnp.where(lane_hit, (p_val * residual)[:, None], 0.0)
+    adjoint = jnp.zeros((rows, LANES), jnp.float32).at[obs_row].add(contrib)
+    adjoint_source = adjoint.reshape(members, slab_rows, plane_cells).astype(jnp.bfloat16)
+
     padded_back = padded_2(adjoint_source, (("gx", 1),), tap_reach)
     x_back = along_x(padded_back, slab_rows).astype(jnp.bfloat16)
     y_back = along_y(x_back).astype(jnp.bfloat16)

time: 601 us -> 302 us (0.50)
  the two profiles are of different devices: /device:TPU:29 before, /device:TPU:2 now
where the time goes in v1:
time: 302 us
  blocking collectives  136 us (45%)
  local copies, waits for them, and re-layouts  49 us (16%)
  waiting for transfers between devices  45.5 us (15%)
  other arithmetic  29.9 us (10%)
  starting transfers between devices  28.6 us (9%)
  matrix products  12.1 us (4%)
    psum x1, blocking collectives, local(): sampled = lax.psum(p_val * s_val, 'mem')  136 us
    scatter-add x1, other arithmetic, local(): adjoint = jnp.zeros((rows, LANES), jnp.float32).at[obs_row].add(contrib)  25.4 us
    ppermute x2, waiting for transfers between devices, padded_2(): lax.ppermute(lax.slice_in_dim(block, block.shape[dim] - width, None, axis...  23.5 us
    ppermute x2, waiting for transfers between devices, padded_2(): lax.ppermute(lax.slice_in_dim(block, 0, width, axis=dim), axis, backward)  22 us
    ppermute x2, starting transfers between devices, padded_2(): lax.ppermute(lax.slice_in_dim(block, 0, width, axis=dim), axis, backward)  21.9 us
    gather x1, local copies, waits for them, and re-layouts, local(): perturbations.reshape(slot_count * rows, LANES)[obs_slot * rows + obs_row]  15 us
    gather x1, local copies, waits for them, and re-layouts, local(): s_rows = smoothed.reshape(rows, LANES)[obs_row]  14.2 us
    ppermute x2, starting transfers between devices, padded_2(): lax.ppermute(lax.slice_in_dim(block, block.shape[dim] - width, None, axis...  6.69 us
  transfers between devices with their start and end apart: 4, of which 4 were waited for; matrix products, arithmetic and copies ran while one was open for 6% of the time, Pallas kernels for 0%

profile of v1, /device:TPU:2, one launch (start us, length us, event | category | flops | bytes accessed | tf_op | source)
XLA Modules:
  0.0 301.9 jit_solution(14526492323340186401)
XLA Ops:
  0.0 0.0 copy-start.4
  0.0 0.0 copy-start.2
  0.0 3.1 %reshape.82 = bf16[16,512,64]{2,1,0:T(8,128)(2,1)S(1)} reshape(bf16[1,16,32768]{2,1,0:T(8,128)(2,1)} %param.13) | data formatting | bytes 2097152 | tf_op jit(solution)/shard_map/reshape
  3.1 0.0 copy-done.4
  3.1 0.0 copy-done.2
  3.1 2.4 fusion.14
  5.5 2.0 copy.15
  7.6 1.7 convert_element_type.82
  9.3 1.5 fusion.25
  10.8 3.8 %collective-permute-start = (bf16[1,15,32768]{2,1,0:T(8,128)(2,1)}, bf16[1,15,32768]{2,1,0:T(8,128)(2,1)}, u32[]{:S(2)}, u32[]{:S(2)}) collective-permute-start(bf16[1,15,32768]{2,1,0:T(8,128)(2,1)} %get-tuple-element.11), channel_id=1, source_target_pairs={{0,1},{1,2},{2,3},{3,4},{4,5},{5,6},{6,7},{7,8},{8,9},{9,10},{10,1... | collective-permute-start | bytes 2949128 | tf_op jit(solution)/shard_map/ppermute | solution.py:21
  14.6 0.0 copy-start.7
  14.7 0.0 copy-start.8
  14.7 11.2 %collective-permute-start.1 = (bf16[1,15,32768]{2,1,0:T(8,128)(2,1)}, bf16[1,15,32768]{2,1,0:T(8,128)(2,1)}, u32[]{:S(2)}, u32[]{:S(2)}) collective-permute-start(bf16[1,15,32768]{2,1,0:T(8,128)(2,1)} %get-tuple-element.12), channel_id=1, source_target_pairs={{1,0},{2,1},{3,2},{4,3},{5,4},{6,5},{7,6},{8,7},{9,8},{10,9},{11,1... | collective-permute-start | bytes 2949128 | tf_op jit(solution)/shard_map/ppermute | solution.py:24
  25.9 2.9 reshape.81
  29.4 0.0 copy-done.7
  29.4 0.0 copy-done.8
  29.5 0.0 copy-start.9
  29.5 15.0 %gather_fusion = bf16[4096,128]{1,0:T(8,128)(2,1)} fusion(bf16[8192,128]{1,0:T(8,128)(2,1)S(1)} %reshape.81, s32[4096]{0:T(1024)S(1)} %get-tuple-element.13), kind=kCustom, calls=%fused_computation | custom fusion | bytes 2113536 | tf_op jit(solution)/shard_map/gather | solution.py:81
  44.5 3.8 %collective-permute-done = bf16[1,15,32768]{2,1,0:T(8,128)(2,1)} collective-permute-done((bf16[1,15,32768]{2,1,0:T(8,128)(2,1)}, bf16[1,15,32768]{2,1,0:T(8,128)(2,1)}, u32[]{:S(2)}, u32[]{:S(2)}) %collective-permute-start) | collective-permute-done | bytes 983072 | tf_op jit(solution)/shard_map/ppermute | solution.py:21
  48.3 15.8 %collective-permute-done.1 = bf16[1,15,32768]{2,1,0:T(8,128)(2,1)} collective-permute-done((bf16[1,15,32768]{2,1,0:T(8,128)(2,1)}, bf16[1,15,32768]{2,1,0:T(8,128)(2,1)}, u32[]{:S(2)}, u32[]{:S(2)}) %collective-permute-start.1) | collective-permute-done | bytes 983072 | tf_op jit(solution)/shard_map/ppermute | solution.py:24
  64.2 0.0 copy-done.9
  64.2 3.8 %convolution_bitcast_fusion = f32[1,16,32768]{2,1,0:T(8,128)} fusion(bf16[16,46]{1,0:T(8,128)(2,1)S(1)} %copy-done.9, bf16[1,15,32768]{2,1,0:T(8,128)(2,1)} %collective-permute-done.1, bf16[1,16,32768]{2,1,0:T(8,128)(2,1)S(1)} %convert_element_type.82, bf16[1,15,32768]{2,1,0:T(8,128)(2,1)} %collective-permute-done), kind=kOutput, calls=%fused_computation.3 | convolution fusion | flops 57278464 | bytes 5113280 | tf_op jit(solution)/shard_map/ip,mpc->mic/dot_general | solution.py:64
  68.0 1.7 reshape.84
  69.7 0.0 copy-start.1
  69.7 14.2 %gather_fusion.1 = f32[4096,128]{1,0:T(8,128)} fusion(f32[4096,128]{1,0:T(8,128)S(1)} %reshape.84, s32[4096]{0:T(1024)S(1)} %get-tuple-element.7), kind=kCustom, calls=%fused_computation.1 | custom fusion | bytes 4210688 | tf_op jit(solution)/shard_map/gather | solution.py:79
  83.9 0.0 copy-start.5
  83.9 0.0 copy-start.6
  83.9 0.0 copy-done.1
  83.9 2.8 select_reduce_fusion
  86.8 136.0 %psum.7 = f32[4096]{0:T(1024)S(1)} all-reduce(f32[4096]{0:T(1024)S(1)} %mul.17), channel_id=1, replica_groups=mesh['mem'=16,'gx'=32] {'mem'}, use_global_device_ids=true, to_apply=%region_2.3 | all-reduce | flops 4096 | bytes 32768 | tf_op jit(solution)/shard_map/psum | solution.py:83
  222.8 0.0 copy-done.5
  222.8 0.0 copy-done.6
  222.8 25.4 %scatter_custom_fusion = f32[4096,128]{1,0:T(8,128)S(1)} fusion(s32[4096]{0:T(1024)S(1)} %get-tuple-element.8, f32[4096]{0:T(1024)S(1)} %multiply_multiply_fusion, s32[4096]{0:T(1024)S(1)} %get-tuple-element.14, f32[]{:T(128)} %constant.34.clone.1), kind=kCustom, calls=%fused_computation.20 | custom fusion | flops 1572864 | bytes 2130944 | tf_op jit(solution)/shard_map/scatter-add | solution.py:88
  248.2 0.1 convert_element_type.83
  248.3 0.5 convert_element_type.84
  248.8 0.2 fusion.24
  249.1 2.9 collective-permute-start.2
  251.9 10.7 %collective-permute-start.3 = (bf16[1,15,32768]{2,1,0:T(8,128)(2,1)S(1)}, bf16[1,15,32768]{2,1,0:T(8,128)(2,1)S(1)}, u32[]{:S(2)}, u32[]{:S(2)}) collective-permute-start(bf16[1,15,32768]{2,1,0:T(8,128)(2,1)S(1)} %get-tuple-element.10), channel_id=1, source_target_pairs={{1,0},{2,1},{3,2},{4,3},{5,4},{6,5},{7,6},{8,7},{9,8},{10,9},{11,1... | collective-permute-start | bytes 2949128 | tf_op jit(solution)/shard_map/ppermute | solution.py:24
  262.6 19.7 %collective-permute-done.2 = bf16[1,15,32768]{2,1,0:T(8,128)(2,1)S(1)} collective-permute-done((bf16[1,15,32768]{2,1,0:T(8,128)(2,1)S(1)}, bf16[1,15,32768]{2,1,0:T(8,128)(2,1)S(1)}, u32[]{:S(2)}, u32[]{:S(2)}) %collective-permute-start.2) | collective-permute-done | bytes 983072 | tf_op jit(solution)/shard_map/ppermute | solution.py:21
  282.3 6.2 %collective-permute-done.3 = bf16[1,15,32768]{2,1,0:T(8,128)(2,1)S(1)} collective-permute-done((bf16[1,15,32768]{2,1,0:T(8,128)(2,1)S(1)}, bf16[1,15,32768]{2,1,0:T(8,128)(2,1)S(1)}, u32[]{:S(2)}, u32[]{:S(2)}) %collective-permute-start.3) | collective-permute-done | bytes 983072 | tf_op jit(solution)/shard_map/ppermute | solution.py:24
  288.4 2.0 fusion
  290.4 0.0 copy-start.3
  290.4 3.1 %reshape.86 = bf16[16,512,64]{2,1,0:T(8,128)(2,1)S(1)} reshape(bf16[1,16,32768]{2,1,0:T(8,128)(2,1)} %fusion) | data formatting | bytes 2097152 | tf_op jit(solution)/shard_map/reshape.9
  293.5 0.0 copy-done.3
  293.5 3.8 %fusion.15 = f32[16,512,64]{2,1,0:T(8,128)} fusion(bf16[64,64,1]{1,0,2:T(8,128)(2,1)S(1)} %copy-done.4, bf16[16,512,64]{2,1,0:T(8,128)(2,1)S(1)} %reshape.86, bf16[512,512,1]{1,0,2:T(8,128)(2,1)S(1)} %copy-done.3), kind=kOutput, calls=%fused_computation.28 | convolution fusion | flops 604504064 | bytes 3678208 | tf_op jit(solution)/shard_map/mxyq,zq->mxyz/dot_general | solution.py:50
  297.4 3.0 reshape.88
  300.4 0.0 copy-done
  300.4 1.5 convert_add_fusion
  (4 shorter events, 0.0 us)
Async XLA Ops:
  0.0 3.1 %copy-start.4 = (bf16[64,64,1]{1,0,2:T(8,128)(2,1)S(1)}, bf16[64,64,1]{1,0,2:T(8,128)(2,1)}, u32[]{:S(2)}) copy-start(bf16[64,64,1]{1,0,2:T(8,128)(2,1)} %constant.49) | copy-start | bytes 24580
  0.0 3.1 %copy-start.2 = (bf16[512,512,1]{1,0,2:T(8,128)(2,1)S(1)}, bf16[512,512,1]{1,0,2:T(8,128)(2,1)}, u32[]{:S(2)}) copy-start(bf16[512,512,1]{1,0,2:T(8,128)(2,1)} %constant.50) | copy-start | bytes 1572868
  10.8 37.5 %collective-permute-start = (bf16[1,15,32768]{2,1,0:T(8,128)(2,1)}, bf16[1,15,32768]{2,1,0:T(8,128)(2,1)}, u32[]{:S(2)}, u32[]{:S(2)}) collective-permute-start(bf16[1,15,32768]{2,1,0:T(8,128)(2,1)} %get-tuple-element.11), channel_id=1, source_target_pairs={{0,1},{1,2},{2,3},{3,4},{4,5},{5,6},{6,7},{7,8},{8,9},{9,10},{10,1... | collective-permute-start | bytes 2949128 | tf_op jit(solution)/shard_map/ppermute | solution.py:21
  14.6 14.8 %copy-start.7 = (s32[4096]{0:T(1024)S(1)}, s32[4096]{0:T(1024)}, u32[]{:S(2)}) copy-start(s32[4096]{0:T(1024)} %param.15) | copy-start | bytes 49156
  14.7 14.8 %copy-start.8 = (s32[4096]{0:T(1024)S(1)}, s32[4096]{0:T(1024)}, u32[]{:S(2)}) copy-start(s32[4096]{0:T(1024)} %param.16) | copy-start | bytes 49156
  14.7 49.5 %collective-permute-start.1 = (bf16[1,15,32768]{2,1,0:T(8,128)(2,1)}, bf16[1,15,32768]{2,1,0:T(8,128)(2,1)}, u32[]{:S(2)}, u32[]{:S(2)}) collective-permute-start(bf16[1,15,32768]{2,1,0:T(8,128)(2,1)} %get-tuple-element.12), channel_id=1, source_target_pairs={{1,0},{2,1},{3,2},{4,3},{5,4},{6,5},{7,6},{8,7},{9,8},{10,9},{11,1... | collective-permute-start | bytes 2949128 | tf_op jit(solution)/shard_map/ppermute | solution.py:24
  29.5 34.7 %copy-start.9 = (bf16[16,46]{1,0:T(8,128)(2,1)S(1)}, bf16[16,46]{1,0:T(8,128)(2,1)}, u32[]{:S(2)}) copy-start(bf16[16,46]{1,0:T(8,128)(2,1)} %constant.45.clone) | copy-start | bytes 4420
  69.7 14.2 %copy-start.1 = (bf16[4096,128]{1,0:T(8,128)(2,1)S(1)}, bf16[4096,128]{1,0:T(8,128)(2,1)}, u32[]{:S(2)}) copy-start(bf16[4096,128]{1,0:T(8,128)(2,1)} %gather_fusion) | copy-start | bytes 3145732
  83.9 138.8 %copy-start.5 = (f32[4096]{0:T(1024)S(1)}, f32[4096]{0:T(1024)}, u32[]{:S(2)}) copy-start(f32[4096]{0:T(1024)} %param.17) | copy-start | bytes 49156
  83.9 138.8 %copy-start.6 = (f32[4096]{0:T(1024)S(1)}, f32[4096]{0:T(1024)}, u32[]{:S(2)}) copy-start(f32[4096]{0:T(1024)} %param.18) | copy-start | bytes 49156
  249.1 33.2 %collective-permute-start.2 = (bf16[1,15,32768]{2,1,0:T(8,128)(2,1)S(1)}, bf16[1,15,32768]{2,1,0:T(8,128)(2,1)S(1)}, u32[]{:S(2)}, u32[]{:S(2)}) collective-permute-start(bf16[1,15,32768]{2,1,0:T(8,128)(2,1)S(1)} %get-tuple-element.9), channel_id=1, source_target_pairs={{0,1},{1,2},{2,3},{3,4},{4,5},{5,6},{6,7},{7,8},{8,9},{9,10},{10,1... | collective-permute-start | bytes 2949128 | tf_op jit(solution)/shard_map/ppermute | solution.py:21
  251.9 36.5 %collective-permute-start.3 = (bf16[1,15,32768]{2,1,0:T(8,128)(2,1)S(1)}, bf16[1,15,32768]{2,1,0:T(8,128)(2,1)S(1)}, u32[]{:S(2)}, u32[]{:S(2)}) collective-permute-start(bf16[1,15,32768]{2,1,0:T(8,128)(2,1)S(1)} %get-tuple-element.10), channel_id=1, source_target_pairs={{1,0},{2,1},{3,2},{4,3},{5,4},{6,5},{7,6},{8,7},{9,8},{10,9},{11,1... | collective-permute-start | bytes 2949128 | tf_op jit(solution)/shard_map/ppermute | solution.py:24
  290.4 3.1 %copy-start.3 = (bf16[512,512,1]{1,0,2:T(8,128)(2,1)S(1)}, bf16[512,512,1]{1,0,2:T(8,128)(2,1)}, u32[]{:S(2)}) copy-start(bf16[512,512,1]{1,0,2:T(8,128)(2,1)} %constant.50) | copy-start | bytes 1572868
  297.4 3.0 copy-start

commit v2 on v1

--- a/solution.py
+++ b/solution.py
@@ -64,6 +64,16 @@
     return jnp.einsum("ip,mpc->mic", band_x, padded, preferred_element_type=jnp.float32)
 
 
+def butterfly_sum(value, axis):
+    count = lax.axis_size(axis)
+    step = 1
+    while step < count:
+        partner = lax.ppermute(value, axis, [(i, i ^ step) for i in range(count)])
+        value = value + partner
+        step *= 2
+    return value
+
+
 def local(weights, perturbations, obs_cell, obs_slot, innovation, obs_weight, obs_count):
     members, slab_rows, plane_cells = weights.shape
     slot_count = perturbations.shape[0]
@@ -80,7 +90,7 @@
     s_val = jnp.sum(jnp.where(lane_hit, s_rows, 0.0), axis=1)
     p_rows = perturbations.reshape(slot_count * rows, LANES)[obs_slot * rows + obs_row]
     p_val = jnp.sum(jnp.where(lane_hit, p_rows.astype(jnp.float32), 0.0), axis=1)
-    sampled = lax.psum(p_val * s_val, "mem")
+    sampled = butterfly_sum(p_val * s_val, "mem")
 
     live_mask = (jnp.arange(nobs) < obs_count[0]).astype(jnp.float32)
     residual = live_mask * obs_weight * (sampled - innovation)

time: 302 us -> 209 us (0.69)
  the two profiles are of different devices: /device:TPU:2 before, /device:TPU:480 now
where the time goes in v2:
time: 209 us; the launch traced here: 207 us
  waiting for transfers between devices  85.1 us (41%)
  local copies, waits for them, and re-layouts  48.9 us (23%)
  other arithmetic  29.9 us (14%)
  starting transfers between devices  29.7 us (14%)
  matrix products  12.1 us (6%)
    ppermute x2, waiting for transfers between devices, padded_2(): lax.ppermute(lax.slice_in_dim(block, 0, width, axis=dim), axis, backward)  42.6 us
    ppermute x2, waiting for transfers between devices, padded_2(): lax.ppermute(lax.slice_in_dim(block, block.shape[dim] - width, None, axis...  25.4 us
    scatter-add x1, other arithmetic, local(): adjoint = jnp.zeros((rows, LANES), jnp.float32).at[obs_row].add(contrib)  25.4 us
    ppermute x4, waiting for transfers between devices, butterfly_sum(): partner = lax.ppermute(value, axis, [(i, i ^ step) for i in range(count)])  17.1 us
    gather x1, local copies, waits for them, and re-layouts, local(): perturbations.reshape(slot_count * rows, LANES)[obs_slot * rows + obs_row]  14.9 us
    gather x1, local copies, waits for them, and re-layouts, local(): s_rows = smoothed.reshape(rows, LANES)[obs_row]  14.2 us
    ppermute x2, starting transfers between devices, padded_2(): lax.ppermute(lax.slice_in_dim(block, block.shape[dim] - width, None, axis...  13.3 us
    ppermute x4, starting transfers between devices, butterfly_sum(): partner = lax.ppermute(value, axis, [(i, i ^ step) for i in range(count)])  12.4 us
  transfers between devices with their start and end apart: 8, of which 8 were waited for; matrix products, arithmetic and copies ran while one was open for 9% of the time, Pallas kernels for 0%

profile of v2, /device:TPU:480, one launch (start us, length us, event | category | flops | bytes accessed | tf_op | source)
XLA Modules:
  0.0 206.6 jit_solution(9641374672938497668)
XLA Ops:
  0.0 3.1 %reshape.82 = bf16[16,512,64]{2,1,0:T(8,128)(2,1)S(1)} reshape(bf16[1,16,32768]{2,1,0:T(8,128)(2,1)} %param.13) | data formatting | bytes 2097152 | tf_op jit(solution)/shard_map/reshape
  3.1 0.0 copy-done.4
  3.1 0.0 copy-done.2
  3.1 2.4 %fusion.14 = bf16[1,16,512,64]{2,3,1,0:T(8,128)(2,1)} fusion(bf16[512,512,1]{1,0,2:T(8,128)(2,1)S(1)} %copy-done.2, bf16[64,64,1]{1,0,2:T(8,128)(2,1)S(1)} %copy-done.4, bf16[16,512,64]{2,1,0:T(8,128)(2,1)S(1)} %reshape.82), kind=kOutput, calls=%fused_computation.27 | convolution fusion | flops 605028352 | bytes 2629632 | tf_op jit(solution)/shard_map/mxqz,yq->mxyz/dot_general | solution.py:58
  5.5 2.0 copy.15
  7.6 1.7 convert_element_type.82
  9.3 1.5 fusion.25
  10.8 7.7 %collective-permute-start = (bf16[1,15,32768]{2,1,0:T(8,128)(2,1)}, bf16[1,15,32768]{2,1,0:T(8,128)(2,1)}, u32[]{:S(2)}, u32[]{:S(2)}) collective-permute-start(bf16[1,15,32768]{2,1,0:T(8,128)(2,1)} %get-tuple-element.11), channel_id=1, source_target_pairs={{0,1},{1,2},{2,3},{3,4},{4,5},{5,6},{6,7},{7,8},{8,9},{9,10},{10,1... | collective-permute-start | bytes 2949128 | tf_op jit(solution)/shard_map/ppermute | solution.py:21
  18.5 0.0 copy-start.5
  18.6 0.0 copy-start.6
  18.6 1.9 collective-permute-start.1
  20.5 2.9 %reshape.81 = bf16[8192,128]{1,0:T(8,128)(2,1)S(1)} reshape(bf16[2,1,16,32768]{3,2,1,0:T(8,128)(2,1)} %param.14) | data formatting | bytes 4194304 | tf_op jit(solution)/shard_map/reshape | solution.py:91
  23.4 0.0 copy-done.5
  23.4 0.0 copy-done.6
  23.4 0.0 copy-start.9
  23.5 14.9 %gather_fusion = bf16[4096,128]{1,0:T(8,128)(2,1)} fusion(bf16[8192,128]{1,0:T(8,128)(2,1)S(1)} %reshape.81, s32[4096]{0:T(1024)S(1)} %get-tuple-element.13), kind=kCustom, calls=%fused_computation | custom fusion | bytes 2113536 | tf_op jit(solution)/shard_map/gather | solution.py:91
  38.4 4.0 %collective-permute-done = bf16[1,15,32768]{2,1,0:T(8,128)(2,1)} collective-permute-done((bf16[1,15,32768]{2,1,0:T(8,128)(2,1)}, bf16[1,15,32768]{2,1,0:T(8,128)(2,1)}, u32[]{:S(2)}, u32[]{:S(2)}) %collective-permute-start) | collective-permute-done | bytes 983072 | tf_op jit(solution)/shard_map/ppermute | solution.py:21
  42.4 22.8 %collective-permute-done.1 = bf16[1,15,32768]{2,1,0:T(8,128)(2,1)} collective-permute-done((bf16[1,15,32768]{2,1,0:T(8,128)(2,1)}, bf16[1,15,32768]{2,1,0:T(8,128)(2,1)}, u32[]{:S(2)}, u32[]{:S(2)}) %collective-permute-start.1) | collective-permute-done | bytes 983072 | tf_op jit(solution)/shard_map/ppermute | solution.py:24
  65.2 0.0 copy-done.9
  65.2 3.8 %convolution_bitcast_fusion = f32[1,16,32768]{2,1,0:T(8,128)} fusion(bf16[16,46]{1,0:T(8,128)(2,1)S(1)} %copy-done.9, bf16[1,15,32768]{2,1,0:T(8,128)(2,1)} %collective-permute-done.1, bf16[1,16,32768]{2,1,0:T(8,128)(2,1)S(1)} %convert_element_type.82, bf16[1,15,32768]{2,1,0:T(8,128)(2,1)} %collective-permute-done), kind=kOutput, calls=%fused_computation.3 | convolution fusion | flops 57278464 | bytes 5113280 | tf_op jit(solution)/shard_map/ip,mpc->mic/dot_general | solution.py:64
  69.0 1.7 reshape.84
  70.7 0.0 copy-start.1
  70.8 14.2 %gather_fusion.1 = f32[4096,128]{1,0:T(8,128)} fusion(f32[4096,128]{1,0:T(8,128)S(1)} %reshape.84, s32[4096]{0:T(1024)S(1)} %get-tuple-element.7), kind=kCustom, calls=%fused_computation.1 | custom fusion | bytes 4210688 | tf_op jit(solution)/shard_map/gather | solution.py:89
  85.0 0.0 copy-done.1
  85.0 2.8 %select_reduce_fusion = (f32[4096]{0:T(1024)S(1)}, f32[4096]{0:T(1024)S(1)}) fusion(f32[4096,128]{1,0:T(8,128)} %gather_fusion.1, s32[4096]{0:T(1024)S(1)} %get-tuple-element.14, bf16[4096,128]{1,0:T(8,128)(2,1)S(1)} %copy-done.1), kind=kLoop, calls=%fused_computation.16 | loop fusion | flops 3137536 | bytes 3194880 | tf_op jit(solution)/shard_map/reduce_sum | solution.py:90
  87.8 1.9 collective-permute-start.2
  89.7 1.1 collective-permute-done.2
  90.9 3.5 %collective-permute-start.3 = (f32[4096]{0:T(1024)S(1)}, f32[4096]{0:T(1024)S(1)}, u32[]{:S(2)}, u32[]{:S(2)}) collective-permute-start(f32[4096]{0:T(1024)S(1)} %add.42), channel_id=1, source_target_pairs={{0,64},{32,96},{64,0},{96,32},{128,192},{160,224},{192,128},{224,1... | collective-permute-start | bytes 49160 | tf_op jit(solution)/shard_map/ppermute | solution.py:71
  94.4 2.1 %collective-permute-done.3 = f32[4096]{0:T(1024)S(1)} collective-permute-done((f32[4096]{0:T(1024)S(1)}, f32[4096]{0:T(1024)S(1)}, u32[]{:S(2)}, u32[]{:S(2)}) %collective-permute-start.3) | collective-permute-done | bytes 16416 | tf_op jit(solution)/shard_map/ppermute | solution.py:71
  96.5 5.1 %collective-permute-start.4 = (f32[4096]{0:T(1024)S(1)}, f32[4096]{0:T(1024)S(1)}, u32[]{:S(2)}, u32[]{:S(2)}) collective-permute-start(f32[4096]{0:T(1024)S(1)} %add.43), channel_id=1, source_target_pairs={{0,128},{32,160},{64,192},{96,224},{128,0},{160,32},{192,64},{224,... | collective-permute-start | bytes 49160 | tf_op jit(solution)/shard_map/ppermute | solution.py:71
  101.6 2.0 collective-permute-done.4
  103.6 1.9 collective-permute-start.5
  106.2 11.8 %collective-permute-done.5 = f32[4096]{0:T(1024)S(1)} collective-permute-done((f32[4096]{0:T(1024)S(1)}, f32[4096]{0:T(1024)S(1)}, u32[]{:S(2)}, u32[]{:S(2)}) %collective-permute-start.5) | collective-permute-done | bytes 16416 | tf_op jit(solution)/shard_map/ppermute | solution.py:71
  118.0 0.0 copy-done.7
  118.0 0.0 copy-done.8
  118.0 25.4 %scatter_custom_fusion = f32[4096,128]{1,0:T(8,128)S(1)} fusion(s32[4096]{0:T(1024)S(1)} %get-tuple-element.8, f32[4096]{0:T(1024)S(1)} %multiply_multiply_fusion, s32[4096]{0:T(1024)S(1)} %get-tuple-element.14, f32[]{:T(128)} %constant.34.clone.1), kind=kCustom, calls=%fused_computation.20 | custom fusion | flops 1572864 | bytes 2130944 | tf_op jit(solution)/shard_map/scatter-add | solution.py:98
  143.4 0.1 convert_element_type.83
  143.5 0.5 convert_element_type.84
  144.0 0.2 fusion.24
  144.3 5.6 %collective-permute-start.6 = (bf16[1,15,32768]{2,1,0:T(8,128)(2,1)S(1)}, bf16[1,15,32768]{2,1,0:T(8,128)(2,1)S(1)}, u32[]{:S(2)}, u32[]{:S(2)}) collective-permute-start(bf16[1,15,32768]{2,1,0:T(8,128)(2,1)S(1)} %get-tuple-element.9), channel_id=1, source_target_pairs={{0,1},{1,2},{2,3},{3,4},{4,5},{5,6},{6,7},{7,8},{8,9},{9,10},{10,1... | collective-permute-start | bytes 2949128 | tf_op jit(solution)/shard_map/ppermute | solution.py:21
  149.9 2.1 %collective-permute-start.7 = (bf16[1,15,32768]{2,1,0:T(8,128)(2,1)S(1)}, bf16[1,15,32768]{2,1,0:T(8,128)(2,1)S(1)}, u32[]{:S(2)}, u32[]{:S(2)}) collective-permute-start(bf16[1,15,32768]{2,1,0:T(8,128)(2,1)S(1)} %get-tuple-element.10), channel_id=1, source_target_pairs={{1,0},{2,1},{3,2},{4,3},{5,4},{6,5},{7,6},{8,7},{9,8},{10,9},{11,1... | collective-permute-start | bytes 2949128 | tf_op jit(solution)/shard_map/ppermute | solution.py:24
  152.0 21.4 %collective-permute-done.6 = bf16[1,15,32768]{2,1,0:T(8,128)(2,1)S(1)} collective-permute-done((bf16[1,15,32768]{2,1,0:T(8,128)(2,1)S(1)}, bf16[1,15,32768]{2,1,0:T(8,128)(2,1)S(1)}, u32[]{:S(2)}, u32[]{:S(2)}) %collective-permute-start.6) | collective-permute-done | bytes 983072 | tf_op jit(solution)/shard_map/ppermute | solution.py:21
  173.4 19.8 %collective-permute-done.7 = bf16[1,15,32768]{2,1,0:T(8,128)(2,1)S(1)} collective-permute-done((bf16[1,15,32768]{2,1,0:T(8,128)(2,1)S(1)}, bf16[1,15,32768]{2,1,0:T(8,128)(2,1)S(1)}, u32[]{:S(2)}, u32[]{:S(2)}) %collective-permute-start.7) | collective-permute-done | bytes 983072 | tf_op jit(solution)/shard_map/ppermute | solution.py:24
  193.2 2.0 fusion
  195.2 3.1 %reshape.86 = bf16[16,512,64]{2,1,0:T(8,128)(2,1)S(1)} reshape(bf16[1,16,32768]{2,1,0:T(8,128)(2,1)} %fusion) | data formatting | bytes 2097152 | tf_op jit(solution)/shard_map/reshape.9
  198.3 3.8 %fusion.15 = f32[16,512,64]{2,1,0:T(8,128)} fusion(bf16[64,64,1]{1,0,2:T(8,128)(2,1)S(1)} %copy-done.4, bf16[16,512,64]{2,1,0:T(8,128)(2,1)S(1)} %reshape.86, bf16[512,512,1]{1,0,2:T(8,128)(2,1)S(1)} %copy-done.3), kind=kOutput, calls=%fused_computation.28 | convolution fusion | flops 604504064 | bytes 3678208 | tf_op jit(solution)/shard_map/mxyq,zq->mxyz/dot_general | solution.py:50
  202.1 3.0 %reshape.88 = f32[1,16,32768]{2,1,0:T(8,128)S(1)} reshape(f32[16,512,64]{2,1,0:T(8,128)} %fusion.15) | data formatting | bytes 4194304 | tf_op jit(solution)/shard_map/reshape | solution.py:51
  205.2 1.5 convert_add_fusion
  (14 shorter events, 0.1 us)
Async XLA Ops:
  0.0 3.1 %copy-start.4 = (bf16[64,64,1]{1,0,2:T(8,128)(2,1)S(1)}, bf16[64,64,1]{1,0,2:T(8,128)(2,1)}, u32[]{:S(2)}) copy-start(bf16[64,64,1]{1,0,2:T(8,128)(2,1)} %constant.49) | copy-start | bytes 24580
  0.0 3.1 %copy-start.2 = (bf16[512,512,1]{1,0,2:T(8,128)(2,1)S(1)}, bf16[512,512,1]{1,0,2:T(8,128)(2,1)}, u32[]{:S(2)}) copy-start(bf16[512,512,1]{1,0,2:T(8,128)(2,1)} %constant.50) | copy-start | bytes 1572868
  10.8 31.6 %collective-permute-start = (bf16[1,15,32768]{2,1,0:T(8,128)(2,1)}, bf16[1,15,32768]{2,1,0:T(8,128)(2,1)}, u32[]{:S(2)}, u32[]{:S(2)}) collective-permute-start(bf16[1,15,32768]{2,1,0:T(8,128)(2,1)} %get-tuple-element.11), channel_id=1, source_target_pairs={{0,1},{1,2},{2,3},{3,4},{4,5},{5,6},{6,7},{7,8},{8,9},{9,10},{10,1... | collective-permute-start | bytes 2949128 | tf_op jit(solution)/shard_map/ppermute | solution.py:21
  18.5 4.8 %copy-start.5 = (s32[4096]{0:T(1024)S(1)}, s32[4096]{0:T(1024)}, u32[]{:S(2)}) copy-start(s32[4096]{0:T(1024)} %param.15) | copy-start | bytes 49156
  18.6 4.8 %copy-start.6 = (s32[4096]{0:T(1024)S(1)}, s32[4096]{0:T(1024)}, u32[]{:S(2)}) copy-start(s32[4096]{0:T(1024)} %param.16) | copy-start | bytes 49156
  18.6 46.6 %collective-permute-start.1 = (bf16[1,15,32768]{2,1,0:T(8,128)(2,1)}, bf16[1,15,32768]{2,1,0:T(8,128)(2,1)}, u32[]{:S(2)}, u32[]{:S(2)}) collective-permute-start(bf16[1,15,32768]{2,1,0:T(8,128)(2,1)} %get-tuple-element.12), channel_id=1, source_target_pairs={{1,0},{2,1},{3,2},{4,3},{5,4},{6,5},{7,6},{8,7},{9,8},{10,9},{11,1... | collective-permute-start | bytes 2949128 | tf_op jit(solution)/shard_map/ppermute | solution.py:24
  23.4 41.8 %copy-start.9 = (bf16[16,46]{1,0:T(8,128)(2,1)S(1)}, bf16[16,46]{1,0:T(8,128)(2,1)}, u32[]{:S(2)}) copy-start(bf16[16,46]{1,0:T(8,128)(2,1)} %constant.45.clone) | copy-start | bytes 4420
  70.7 14.2 %copy-start.1 = (bf16[4096,128]{1,0:T(8,128)(2,1)S(1)}, bf16[4096,128]{1,0:T(8,128)(2,1)}, u32[]{:S(2)}) copy-start(bf16[4096,128]{1,0:T(8,128)(2,1)} %gather_fusion) | copy-start | bytes 3145732
  85.0 33.0 %copy-start.7 = (f32[4096]{0:T(1024)S(1)}, f32[4096]{0:T(1024)}, u32[]{:S(2)}) copy-start(f32[4096]{0:T(1024)} %param.17) | copy-start | bytes 49156
  85.0 33.0 %copy-start.8 = (f32[4096]{0:T(1024)S(1)}, f32[4096]{0:T(1024)}, u32[]{:S(2)}) copy-start(f32[4096]{0:T(1024)} %param.18) | copy-start | bytes 49156
  87.8 3.1 %collective-permute-start.2 = (f32[4096]{0:T(1024)S(1)}, f32[4096]{0:T(1024)S(1)}, u32[]{:S(2)}, u32[]{:S(2)}) collective-permute-start(f32[4096]{0:T(1024)S(1)} %mul.17), channel_id=1, source_target_pairs={{0,32},{32,0},{64,96},{96,64},{128,160},{160,128},{192,224},{224,1... | collective-permute-start | bytes 49160 | tf_op jit(solution)/shard_map/ppermute | solution.py:71
  90.9 5.6 %collective-permute-start.3 = (f32[4096]{0:T(1024)S(1)}, f32[4096]{0:T(1024)S(1)}, u32[]{:S(2)}, u32[]{:S(2)}) collective-permute-start(f32[4096]{0:T(1024)S(1)} %add.42), channel_id=1, source_target_pairs={{0,64},{32,96},{64,0},{96,32},{128,192},{160,224},{192,128},{224,1... | collective-permute-start | bytes 49160 | tf_op jit(solution)/shard_map/ppermute | solution.py:71
  96.5 7.1 %collective-permute-start.4 = (f32[4096]{0:T(1024)S(1)}, f32[4096]{0:T(1024)S(1)}, u32[]{:S(2)}, u32[]{:S(2)}) collective-permute-start(f32[4096]{0:T(1024)S(1)} %add.43), channel_id=1, source_target_pairs={{0,128},{32,160},{64,192},{96,224},{128,0},{160,32},{192,64},{224,... | collective-permute-start | bytes 49160 | tf_op jit(solution)/shard_map/ppermute | solution.py:71
  103.6 14.3 %collective-permute-start.5 = (f32[4096]{0:T(1024)S(1)}, f32[4096]{0:T(1024)S(1)}, u32[]{:S(2)}, u32[]{:S(2)}) collective-permute-start(f32[4096]{0:T(1024)S(1)} %add.44), channel_id=1, source_target_pairs={{0,256},{32,288},{64,320},{96,352},{128,384},{160,416},{192,448},{... | collective-permute-start | bytes 49160 | tf_op jit(solution)/shard_map/ppermute | solution.py:71
  144.3 29.1 %collective-permute-start.6 = (bf16[1,15,32768]{2,1,0:T(8,128)(2,1)S(1)}, bf16[1,15,32768]{2,1,0:T(8,128)(2,1)S(1)}, u32[]{:S(2)}, u32[]{:S(2)}) collective-permute-start(bf16[1,15,32768]{2,1,0:T(8,128)(2,1)S(1)} %get-tuple-element.9), channel_id=1, source_target_pairs={{0,1},{1,2},{2,3},{3,4},{4,5},{5,6},{6,7},{7,8},{8,9},{9,10},{10,1... | collective-permute-start | bytes 2949128 | tf_op jit(solution)/shard_map/ppermute | solution.py:21
  149.9 43.3 %collective-permute-start.7 = (bf16[1,15,32768]{2,1,0:T(8,128)(2,1)S(1)}, bf16[1,15,32768]{2,1,0:T(8,128)(2,1)S(1)}, u32[]{:S(2)}, u32[]{:S(2)}) collective-permute-start(bf16[1,15,32768]{2,1,0:T(8,128)(2,1)S(1)} %get-tuple-element.10), channel_id=1, source_target_pairs={{1,0},{2,1},{3,2},{4,3},{5,4},{6,5},{7,6},{8,7},{9,8},{10,9},{11,1... | collective-permute-start | bytes 2949128 | tf_op jit(solution)/shard_map/ppermute | solution.py:24
  195.2 3.1 %copy-start.3 = (bf16[512,512,1]{1,0,2:T(8,128)(2,1)S(1)}, bf16[512,512,1]{1,0,2:T(8,128)(2,1)}, u32[]{:S(2)}) copy-start(bf16[512,512,1]{1,0,2:T(8,128)(2,1)} %constant.50) | copy-start | bytes 1572868
  202.1 3.0 %copy-start = (bf16[1,16,32768]{2,1,0:T(8,128)(2,1)S(1)}, bf16[1,16,32768]{2,1,0:T(8,128)(2,1)}, u32[]{:S(2)}) copy-start(bf16[1,16,32768]{2,1,0:T(8,128)(2,1)} %param.13) | copy-start | bytes 3145732

commit v3 on v2

--- a/solution.py
+++ b/solution.py
@@ -3,6 +3,8 @@
 import jax.numpy as jnp
 from jax import lax
 from jax.sharding import PartitionSpec as P
+from jax.experimental import pallas as pl
+from jax.experimental.pallas import tpu as pltpu
 
 NY = 512
 NZ = 64
@@ -74,6 +76,85 @@
     return value
 
 
+def gather_rows(index, field):
+    count = index.shape[0]
+    field_rows = field.shape[0]
+
+    def kernel(index_ref, field_ref, out_ref):
+        def body(i, carry):
+            row = jnp.clip(index_ref[i], 0, field_rows - 1)
+            out_ref[pl.ds(i, 1), :] = field_ref[pl.ds(row, 1), :]
+            return carry
+
+        lax.fori_loop(0, count, body, 0, unroll=8)
+
+    return pl.pallas_call(
+        kernel,
+        out_shape=jax.ShapeDtypeStruct((count, LANES), field.dtype),
+        grid_spec=pltpu.PrefetchScalarGridSpec(
+            num_scalar_prefetch=1,
+            grid=(1,),
+            in_specs=[pl.BlockSpec(field.shape, lambda i, index: (0, 0))],
+            out_specs=pl.BlockSpec((count, LANES), lambda i, index: (0, 0)),
+        ),
+        compiler_params=pltpu.CompilerParams(vmem_limit_bytes=40 * 1024 * 1024),
+    )(index, field)
+
+
+def scatter_regions(index, update, region_rows, splits):
+    regions = len(region_rows)
+    per_region = index.shape[0] // regions
+    per_stream = per_region // splits
+    total_rows = sum(region_rows)
+
+    def kernel(index_ref, update_ref, out_ref, *accs):
+        for acc in accs:
+            acc[...] = jnp.zeros_like(acc)
+
+        def body(j, carry):
+            for region in range(regions):
+                for split in range(splits):
+                    i = region * per_region + split * per_stream + j
+                    row = jnp.clip(index_ref[i], 0, region_rows[region])
+                    acc = accs[region * splits + split]
+                    acc[pl.ds(row, 1), :] += update_ref[pl.ds(i, 1), :]
+            return carry
+
+        lax.fori_loop(0, per_stream, body, 0, unroll=2)
+        start = 0
+        for region in range(regions):
+            size = region_rows[region]
+            total = accs[region * splits][0:size, :]
+            for split in range(1, splits):
+                total = total + accs[region * splits + split][0:size, :]
+            out_ref[start:start + size, :] = total.astype(out_ref.dtype)
+            start += size
+
+    return pl.pallas_call(
+        kernel,
+        out_shape=jax.ShapeDtypeStruct((total_rows, LANES), jnp.bfloat16),
+        grid_spec=pltpu.PrefetchScalarGridSpec(
+            num_scalar_prefetch=1,
+            grid=(1,),
+            in_specs=[pl.BlockSpec(update.shape, lambda i, index: (0, 0))],
+            out_specs=pl.BlockSpec((total_rows, LANES), lambda i, index: (0, 0)),
+            scratch_shapes=[
+                pltpu.VMEM((rows + 8, LANES), jnp.float32)
+                for rows in region_rows
+                for _ in range(splits)
+            ],
+        ),
+        compiler_params=pltpu.CompilerParams(vmem_limit_bytes=48 * 1024 * 1024),
+    )(index, update)
+
+
+def neighbours(value, axis):
+    count = lax.axis_size(axis)
+    from_left = lax.ppermute(value, axis, [(i, i + 1) for i in range(count - 1)])
+    from_right = lax.ppermute(value, axis, [(i + 1, i) for i in range(count - 1)])
+    return from_left, from_right
+
+
 def local(weights, perturbations, obs_cell, obs_slot, innovation, obs_weight, obs_count):
     members, slab_rows, plane_cells = weights.shape
     slot_count = perturbations.shape[0]
@@ -86,7 +167,7 @@
 
     obs_row = obs_cell // LANES
     lane_hit = lax.broadcasted_iota(jnp.int32, (nobs, LANES), 1) == (obs_cell % LANES)[:, None]
-    s_rows = smoothed.reshape(rows, LANES)[obs_row]
+    s_rows = gather_rows(obs_row, smoothed.reshape(rows, LANES))
     s_val = jnp.sum(jnp.where(lane_hit, s_rows, 0.0), axis=1)
     p_rows = perturbations.reshape(slot_count * rows, LANES)[obs_slot * rows + obs_row]
     p_val = jnp.sum(jnp.where(lane_hit, p_rows.astype(jnp.float32), 0.0), axis=1)
@@ -94,11 +175,25 @@
 
     live_mask = (jnp.arange(nobs) < obs_count[0]).astype(jnp.float32)
     residual = live_mask * obs_weight * (sampled - innovation)
-    contrib = jnp.where(lane_hit, (p_val * residual)[:, None], 0.0)
-    adjoint = jnp.zeros((rows, LANES), jnp.float32).at[obs_row].add(contrib)
-    adjoint_source = adjoint.reshape(members, slab_rows, plane_cells).astype(jnp.bfloat16)
-
-    padded_back = padded_2(adjoint_source, (("gx", 1),), tap_reach)
+    contrib = p_val * residual
+
+    plane_rows = plane_cells // LANES
+    halo_rows = tap_reach * plane_rows
+    left_cell, right_cell = neighbours(obs_cell, "gx")
+    left_contrib, right_contrib = neighbours(contrib, "gx")
+    left_row = jnp.where(
+        left_cell >= (slab_rows - tap_reach) * plane_cells,
+        left_cell // LANES - (slab_rows - tap_reach) * plane_rows,
+        halo_rows,
+    )
+    right_row = jnp.where(right_cell < tap_reach * plane_cells, right_cell // LANES, halo_rows)
+    all_cell = jnp.concatenate([left_cell, obs_cell, right_cell])
+    all_row = jnp.concatenate([left_row, obs_row, right_row])
+    all_contrib = jnp.concatenate([left_contrib, contrib, right_contrib])
+    all_hit = lax.broadcasted_iota(jnp.int32, (3 * nobs, LANES), 1) == (all_cell % LANES)[:, None]
+    update = jnp.where(all_hit, all_contrib[:, None], 0.0)
+    extended = scatter_regions(all_row, update, (halo_rows, rows, halo_rows), 2)
+    padded_back = extended.reshape(members, slab_rows + 2 * tap_reach, plane_cells)
     x_back = along_x(padded_back, slab_rows).astype(jnp.bfloat16)
     y_back = along_y(x_back).astype(jnp.bfloat16)
     return weights.astype(jnp.float32) + along_z(y_back)

time: 209 us -> 212 us (1.014)
  the two profiles are of different devices: /device:TPU:480 before, /device:TPU:6 now
where the time goes in v3:
time: 212 us
  waiting for transfers between devices  56.4 us (27%)
  starting transfers between devices  50.3 us (24%)
  Pallas kernels  44.5 us (21%)
  local copies, waits for them, and re-layouts  35.3 us (17%)
  matrix products  13.7 us (6%)
  other arithmetic  10.4 us (5%)
    ppermute x2, waiting for transfers between devices, neighbours(): lax.ppermute(value, axis, [(i, i + 1) for i in range(count - 1)])  50.5 us
    pallas_call x1, Pallas kernels, scatter_regions(): pl.pallas_call(kernel, out_shape=jax.ShapeDtypeStruct((total_rows, LANES)...  32.9 us
    ppermute x4, starting transfers between devices, butterfly_sum(): partner = lax.ppermute(value, axis, [(i, i ^ step) for i in range(count)])  22 us
    gather x1, local copies, waits for them, and re-layouts, local(): perturbations.reshape(slot_count * rows, LANES)[obs_slot * rows + obs_row]  14.9 us
    pallas_call x1, Pallas kernels, gather_rows(): pl.pallas_call(kernel, out_shape=jax.ShapeDtypeStruct((count, LANES), fie...  11.6 us
    ppermute x1, starting transfers between devices, padded_2(): lax.ppermute(lax.slice_in_dim(block, 0, width, axis=dim), axis, backward)  11.5 us
    ppermute x2, starting transfers between devices, neighbours(): lax.ppermute(value, axis, [(i + 1, i) for i in range(count - 1)])  8.97 us
    select_n x1, other arithmetic, local(): update = jnp.where(all_hit, all_contrib[:, None], 0.0)  7.22 us
  transfers between devices with their start and end apart: 10, of which 5 were waited for; matrix products, arithmetic and copies ran while one was open for 8% of the time, Pallas kernels for 0%

profile of v3, /device:TPU:6, one launch (start us, length us, event | category | flops | bytes accessed | tf_op | source)
XLA Modules:
  0.0 211.6 jit_solution(6197889741526216884)
XLA Ops:
  0.0 3.0 %reshape.138 = bf16[16,512,64]{2,1,0:T(8,128)(2,1)S(1)} reshape(bf16[1,16,32768]{2,1,0:T(8,128)(2,1)} %param.13) | data formatting | bytes 2097152 | tf_op jit(solution)/shard_map/reshape
  3.1 0.0 copy-done.2
  3.1 2.5 %fusion.8 = bf16[1,16,512,64]{2,3,1,0:T(8,128)(2,1)S(1)} fusion(bf16[512,512,1]{1,0,2:T(8,128)(2,1)} %constant.80, bf16[64,64,1]{1,0,2:T(8,128)(2,1)S(1)} %copy-done.2, bf16[16,512,64]{2,1,0:T(8,128)(2,1)S(1)} %reshape.138), kind=kOutput, calls=%fused_computation.20 | convolution fusion | flops 605028352 | bytes 2629632 | tf_op jit(solution)/shard_map/mxqz,yq->mxyz/dot_general | solution.py:60
  5.6 1.1 copy.15
  6.7 1.7 convert_element_type.68
  8.3 0.0 copy-start.4
  8.4 1.5 fusion.22
  9.9 3.8 %collective-permute-start.2 = (bf16[1,15,32768]{2,1,0:T(8,128)(2,1)}, bf16[1,15,32768]{2,1,0:T(8,128)(2,1)}, u32[]{:S(2)}, u32[]{:S(2)}) collective-permute-start(bf16[1,15,32768]{2,1,0:T(8,128)(2,1)} %get-tuple-element.7), channel_id=1, source_target_pairs={{0,1},{1,2},{2,3},{3,4},{4,5},{5,6},{6,7},{7,8},{8,9},{9,10},{10,1... | collective-permute-start | bytes 2949128 | tf_op jit(solution)/shard_map/ppermute | solution.py:23
  13.7 0.0 copy-start.3
  13.7 11.5 %collective-permute-start.3 = (bf16[1,15,32768]{2,1,0:T(8,128)(2,1)}, bf16[1,15,32768]{2,1,0:T(8,128)(2,1)}, u32[]{:S(2)}, u32[]{:S(2)}) collective-permute-start(bf16[1,15,32768]{2,1,0:T(8,128)(2,1)} %get-tuple-element.8), channel_id=1, source_target_pairs={{1,0},{2,1},{3,2},{4,3},{5,4},{6,5},{7,6},{8,7},{9,8},{10,9},{11,1... | collective-permute-start | bytes 2949128 | tf_op jit(solution)/shard_map/ppermute | solution.py:26
  25.3 0.0 copy-done.4
  25.3 1.9 collective-permute-start
  27.2 2.9 %reshape.137 = bf16[8192,128]{1,0:T(8,128)(2,1)S(1)} reshape(bf16[2,1,16,32768]{3,2,1,0:T(8,128)(2,1)} %param.14) | data formatting | bytes 4194304 | tf_op jit(solution)/shard_map/reshape | solution.py:172
  30.1 39.5 %collective-permute-done = s32[4096]{0:T(1024)S(1)} collective-permute-done((s32[4096]{0:T(1024)S(1)}, s32[4096]{0:T(1024)S(1)}, u32[]{:S(2)}, u32[]{:S(2)}) %collective-permute-start) | collective-permute-done | bytes 16416 | tf_op jit(solution)/shard_map/ppermute | solution.py:153
  69.6 0.0 copy-start.7
  69.6 14.9 %gather_fusion = bf16[4096,128]{1,0:T(8,128)(2,1)} fusion(bf16[8192,128]{1,0:T(8,128)(2,1)S(1)} %reshape.137, s32[4096]{0:T(1024)S(1)} %get-tuple-element.12), kind=kCustom, calls=%fused_computation | custom fusion | bytes 2113536 | tf_op jit(solution)/shard_map/gather | solution.py:172
  84.5 0.0 collective-permute-done.2
  84.5 0.0 collective-permute-done.3
  84.5 0.0 copy-done.7
  84.5 3.8 %convolution_bitcast_fusion = f32[1,16,32768]{2,1,0:T(8,128)} fusion(bf16[16,46]{1,0:T(8,128)(2,1)S(1)} %copy-done.7, bf16[1,15,32768]{2,1,0:T(8,128)(2,1)} %collective-permute-done.3, bf16[1,16,32768]{2,1,0:T(8,128)(2,1)S(1)} %convert_element_type.68, bf16[1,15,32768]{2,1,0:T(8,128)(2,1)} %collective-permute-done.2), kind=kOutput, calls=%fused_computation.1 | convolution fusion | flops 57278464 | bytes 5113280 | tf_op jit(solution)/shard_map/ip,mpc->mic/dot_general | solution.py:66
  88.4 1.7 reshape.140.field_ref
  90.1 11.6 %shard_map.127 = f32[4096,128]{1,0:T(8,128)S(1)} custom-call(s32[4096]{0:T(1024)S(1)} %get-tuple-element.14.index_ref, f32[4096,128]{1,0:T(8,128)S(1)} %reshape.140.field_ref), custom_call_target="tpu_custom_call" | custom-call | tf_op jit(solution)/shard_map/pallas_call | solution.py:91
  101.7 0.0 copy-start.5
  101.7 0.0 copy-start.6
  101.7 0.0 copy-done.1
  101.7 1.6 select_reduce_fusion
  103.3 1.9 collective-permute-start.4
  105.2 1.1 collective-permute-done.4
  106.4 3.5 %collective-permute-start.5 = (f32[4096]{0:T(1024)S(1)}, f32[4096]{0:T(1024)S(1)}, u32[]{:S(2)}, u32[]{:S(2)}) collective-permute-start(f32[4096]{0:T(1024)S(1)} %add.49), channel_id=1, source_target_pairs={{0,64},{32,96},{64,0},{96,32},{128,192},{160,224},{192,128},{224,1... | collective-permute-start | bytes 49160 | tf_op jit(solution)/shard_map/ppermute | solution.py:73
  109.9 3.6 %collective-permute-start.1 = (s32[4096]{0:T(1024)S(1)}, s32[4096]{0:T(1024)S(1)}, u32[]{:S(2)}, u32[]{:S(2)}) collective-permute-start(s32[4096]{0:T(1024)S(1)} %copy-done.4), channel_id=1, source_target_pairs={{1,0},{2,1},{3,2},{4,3},{5,4},{6,5},{7,6},{8,7},{9,8},{10,9},{11,1... | collective-permute-start | bytes 49160 | tf_op jit(solution)/shard_map/ppermute | solution.py:154
  114.1 0.0 collective-permute-done.5
  114.1 4.8 %collective-permute-start.6 = (f32[4096]{0:T(1024)S(1)}, f32[4096]{0:T(1024)S(1)}, u32[]{:S(2)}, u32[]{:S(2)}) collective-permute-start(f32[4096]{0:T(1024)S(1)} %add.50), channel_id=1, source_target_pairs={{0,128},{32,160},{64,192},{96,224},{128,0},{160,32},{192,64},{224,... | collective-permute-start | bytes 49160 | tf_op jit(solution)/shard_map/ppermute | solution.py:73
  119.0 0.0 collective-permute-done.1
  119.0 2.3 %collective-permute-done.6 = f32[4096]{0:T(1024)S(1)} collective-permute-done((f32[4096]{0:T(1024)S(1)}, f32[4096]{0:T(1024)S(1)}, u32[]{:S(2)}, u32[]{:S(2)}) %collective-permute-start.6) | collective-permute-done | bytes 16416 | tf_op jit(solution)/shard_map/ppermute | solution.py:73
  121.3 11.8 %collective-permute-start.7 = (f32[4096]{0:T(1024)S(1)}, f32[4096]{0:T(1024)S(1)}, u32[]{:S(2)}, u32[]{:S(2)}) collective-permute-start(f32[4096]{0:T(1024)S(1)} %add.51), channel_id=1, source_target_pairs={{0,256},{32,288},{64,320},{96,352},{128,384},{160,416},{192,448},{... | collective-permute-start | bytes 49160 | tf_op jit(solution)/shard_map/ppermute | solution.py:73
  133.1 2.5 %collective-permute-done.7 = f32[4096]{0:T(1024)S(1)} collective-permute-done((f32[4096]{0:T(1024)S(1)}, f32[4096]{0:T(1024)S(1)}, u32[]{:S(2)}, u32[]{:S(2)}) %collective-permute-start.7) | collective-permute-done | bytes 16416 | tf_op jit(solution)/shard_map/ppermute | solution.py:73
  135.6 5.4 %collective-permute-start.9 = (f32[4096]{0:T(1024)S(1)}, f32[4096]{0:T(1024)S(1)}, u32[]{:S(2)}, u32[]{:S(2)}) collective-permute-start(f32[4096]{0:T(1024)S(1)} %multiply_multiply_fusion), channel_id=1, source_target_pairs={{1,0},{2,1},{3,2},{4,3},{5,4},{6,5},{7,6},{8,7},{9,8},{10,9},{11,1... | collective-permute-start | bytes 49160 | tf_op jit(solution)/shard_map/ppermute | solution.py:154
  141.0 2.1 collective-permute-start.8
  143.1 0.0 collective-permute-done.9
  143.1 11.0 %collective-permute-done.8 = f32[4096]{0:T(1024)S(1)} collective-permute-done((f32[4096]{0:T(1024)S(1)}, f32[4096]{0:T(1024)S(1)}, u32[]{:S(2)}, u32[]{:S(2)}) %collective-permute-start.8) | collective-permute-done | bytes 16416 | tf_op jit(solution)/shard_map/ppermute | solution.py:153
  154.2 7.2 %fusion.1.update_ref = f32[12288,128]{1,0:T(8,128)} fusion(f32[12288]{0:T(1024)S(1)} %pad_maximum_fusion, s32[12288]{0:T(1024)S(1)} %add_select_fusion), kind=kLoop, calls=%fused_computation.5 | loop fusion | flops 3145728 | bytes 6389760 | tf_op jit(solution)/shard_map/jit(_where)/select_n | solution.py:194
  161.4 32.9 %shard_map.128 = bf16[11776,128]{1,0:T(8,128)(2,1)S(1)} custom-call(s32[12288]{0:T(1024)S(1)} %pad_add_fusion.index_ref, f32[12288,128]{1,0:T(8,128)} %fusion.1.update_ref), custom_call_target="tpu_custom_call" | custom-call | tf_op jit(solution)/shard_map/pallas_call | solution.py:133
  194.3 3.2 %reshape.141 = bf16[46,32768]{1,0:T(8,128)(2,1)} reshape(bf16[11776,128]{1,0:T(8,128)(2,1)S(1)} %shard_map.128) | data formatting | bytes 6029312 | tf_op jit(solution)/shard_map/reshape.7
  197.5 2.4 %fusion = bf16[1,16,32768]{2,1,0:T(8,128)(2,1)S(1)} fusion(bf16[46,32768]{1,0:T(8,128)(2,1)} %reshape.141, bf16[16,46]{1,0:T(8,128)(2,1)S(1)} %copy-done.7), kind=kOutput, calls=%fused_computation.3 | convolution fusion | flops 48758784 | bytes 4064704 | tf_op jit(solution)/shard_map/ip,mpc->mic/dot_general | solution.py:66
  199.9 2.3 %reshape.142 = bf16[16,512,64]{2,1,0:T(8,128)(2,1)S(1)} reshape(bf16[1,16,32768]{2,1,0:T(8,128)(2,1)S(1)} %fusion) | data formatting | bytes 2097152 | tf_op jit(solution)/shard_map/reshape.9
  202.2 4.9 %fusion.9 = f32[16,512,64]{2,1,0:T(8,128)} fusion(bf16[64,64,1]{1,0,2:T(8,128)(2,1)S(1)} %copy-done.2, bf16[16,512,64]{2,1,0:T(8,128)(2,1)S(1)} %reshape.142, bf16[512,512,1]{1,0,2:T(8,128)(2,1)} %constant.80), kind=kOutput, calls=%fused_computation.21 | convolution fusion | flops 604504064 | bytes 3678208 | tf_op jit(solution)/shard_map/mxyq,zq->mxyz/dot_general | solution.py:52
  207.1 3.0 %reshape.144 = f32[1,16,32768]{2,1,0:T(8,128)S(1)} reshape(f32[16,512,64]{2,1,0:T(8,128)} %fusion.9) | data formatting | bytes 4194304 | tf_op jit(solution)/shard_map/reshape | solution.py:53
  210.1 1.5 convert_add_fusion
  (18 shorter events, 0.1 us)
Async XLA Ops:
  0.0 3.1 %copy-start.2 = (bf16[64,64,1]{1,0,2:T(8,128)(2,1)S(1)}, bf16[64,64,1]{1,0,2:T(8,128)(2,1)}, u32[]{:S(2)}) copy-start(bf16[64,64,1]{1,0,2:T(8,128)(2,1)} %constant.79) | copy-start | bytes 24580
  8.3 16.9 %copy-start.4 = (s32[4096]{0:T(1024)S(1)}, s32[4096]{0:T(1024)}, u32[]{:S(2)}) copy-start(s32[4096]{0:T(1024)} %param.15) | copy-start | bytes 49156
  9.9 74.6 %collective-permute-start.2 = (bf16[1,15,32768]{2,1,0:T(8,128)(2,1)}, bf16[1,15,32768]{2,1,0:T(8,128)(2,1)}, u32[]{:S(2)}, u32[]{:S(2)}) collective-permute-start(bf16[1,15,32768]{2,1,0:T(8,128)(2,1)} %get-tuple-element.7), channel_id=1, source_target_pairs={{0,1},{1,2},{2,3},{3,4},{4,5},{5,6},{6,7},{7,8},{8,9},{9,10},{10,1... | collective-permute-start | bytes 2949128 | tf_op jit(solution)/shard_map/ppermute | solution.py:23
  13.7 55.8 %copy-start.3 = (s32[4096]{0:T(1024)S(1)}, s32[4096]{0:T(1024)}, u32[]{:S(2)}) copy-start(s32[4096]{0:T(1024)} %param.16) | copy-start | bytes 49156
  13.7 70.8 %collective-permute-start.3 = (bf16[1,15,32768]{2,1,0:T(8,128)(2,1)}, bf16[1,15,32768]{2,1,0:T(8,128)(2,1)}, u32[]{:S(2)}, u32[]{:S(2)}) collective-permute-start(bf16[1,15,32768]{2,1,0:T(8,128)(2,1)} %get-tuple-element.8), channel_id=1, source_target_pairs={{1,0},{2,1},{3,2},{4,3},{5,4},{6,5},{7,6},{8,7},{9,8},{10,9},{11,1... | collective-permute-start | bytes 2949128 | tf_op jit(solution)/shard_map/ppermute | solution.py:26
  25.3 44.3 %collective-permute-start = (s32[4096]{0:T(1024)S(1)}, s32[4096]{0:T(1024)S(1)}, u32[]{:S(2)}, u32[]{:S(2)}) collective-permute-start(s32[4096]{0:T(1024)S(1)} %copy-done.4), channel_id=1, source_target_pairs={{0,1},{1,2},{2,3},{3,4},{4,5},{5,6},{6,7},{7,8},{8,9},{9,10},{10,1... | collective-permute-start | bytes 49160 | tf_op jit(solution)/shard_map/ppermute | solution.py:153
  69.6 14.9 %copy-start.7 = (bf16[16,46]{1,0:T(8,128)(2,1)S(1)}, bf16[16,46]{1,0:T(8,128)(2,1)}, u32[]{:S(2)}) copy-start(bf16[16,46]{1,0:T(8,128)(2,1)} %constant.75.clone) | copy-start | bytes 4420
  90.1 11.6 %copy-start.1 = (bf16[4096,128]{1,0:T(8,128)(2,1)S(1)}, bf16[4096,128]{1,0:T(8,128)(2,1)}, u32[]{:S(2)}) copy-start(bf16[4096,128]{1,0:T(8,128)(2,1)} %gather_fusion) | copy-start | bytes 3145732
  101.7 33.9 %copy-start.5 = (f32[4096]{0:T(1024)S(1)}, f32[4096]{0:T(1024)}, u32[]{:S(2)}) copy-start(f32[4096]{0:T(1024)} %param.17) | copy-start | bytes 49156
  101.7 33.9 %copy-start.6 = (f32[4096]{0:T(1024)S(1)}, f32[4096]{0:T(1024)}, u32[]{:S(2)}) copy-start(f32[4096]{0:T(1024)} %param.18) | copy-start | bytes 49156
  103.3 3.1 %collective-permute-start.4 = (f32[4096]{0:T(1024)S(1)}, f32[4096]{0:T(1024)S(1)}, u32[]{:S(2)}, u32[]{:S(2)}) collective-permute-start(f32[4096]{0:T(1024)S(1)} %mul.21), channel_id=1, source_target_pairs={{0,32},{32,0},{64,96},{96,64},{128,160},{160,128},{192,224},{224,1... | collective-permute-start | bytes 49160 | tf_op jit(solution)/shard_map/ppermute | solution.py:73
  106.4 7.7 %collective-permute-start.5 = (f32[4096]{0:T(1024)S(1)}, f32[4096]{0:T(1024)S(1)}, u32[]{:S(2)}, u32[]{:S(2)}) collective-permute-start(f32[4096]{0:T(1024)S(1)} %add.49), channel_id=1, source_target_pairs={{0,64},{32,96},{64,0},{96,32},{128,192},{160,224},{192,128},{224,1... | collective-permute-start | bytes 49160 | tf_op jit(solution)/shard_map/ppermute | solution.py:73
  109.9 9.1 %collective-permute-start.1 = (s32[4096]{0:T(1024)S(1)}, s32[4096]{0:T(1024)S(1)}, u32[]{:S(2)}, u32[]{:S(2)}) collective-permute-start(s32[4096]{0:T(1024)S(1)} %copy-done.4), channel_id=1, source_target_pairs={{1,0},{2,1},{3,2},{4,3},{5,4},{6,5},{7,6},{8,7},{9,8},{10,9},{11,1... | collective-permute-start | bytes 49160 | tf_op jit(solution)/shard_map/ppermute | solution.py:154
  114.1 7.1 %collective-permute-start.6 = (f32[4096]{0:T(1024)S(1)}, f32[4096]{0:T(1024)S(1)}, u32[]{:S(2)}, u32[]{:S(2)}) collective-permute-start(f32[4096]{0:T(1024)S(1)} %add.50), channel_id=1, source_target_pairs={{0,128},{32,160},{64,192},{96,224},{128,0},{160,32},{192,64},{224,... | collective-permute-start | bytes 49160 | tf_op jit(solution)/shard_map/ppermute | solution.py:73
  121.3 14.3 %collective-permute-start.7 = (f32[4096]{0:T(1024)S(1)}, f32[4096]{0:T(1024)S(1)}, u32[]{:S(2)}, u32[]{:S(2)}) collective-permute-start(f32[4096]{0:T(1024)S(1)} %add.51), channel_id=1, source_target_pairs={{0,256},{32,288},{64,320},{96,352},{128,384},{160,416},{192,448},{... | collective-permute-start | bytes 49160 | tf_op jit(solution)/shard_map/ppermute | solution.py:73
  135.6 7.5 %collective-permute-start.9 = (f32[4096]{0:T(1024)S(1)}, f32[4096]{0:T(1024)S(1)}, u32[]{:S(2)}, u32[]{:S(2)}) collective-permute-start(f32[4096]{0:T(1024)S(1)} %multiply_multiply_fusion), channel_id=1, source_target_pairs={{1,0},{2,1},{3,2},{4,3},{5,4},{6,5},{7,6},{8,7},{9,8},{10,9},{11,1... | collective-permute-start | bytes 49160 | tf_op jit(solution)/shard_map/ppermute | solution.py:154
  141.0 13.1 %collective-permute-start.8 = (f32[4096]{0:T(1024)S(1)}, f32[4096]{0:T(1024)S(1)}, u32[]{:S(2)}, u32[]{:S(2)}) collective-permute-start(f32[4096]{0:T(1024)S(1)} %multiply_multiply_fusion), channel_id=1, source_target_pairs={{0,1},{1,2},{2,3},{3,4},{4,5},{5,6},{6,7},{7,8},{8,9},{9,10},{10,1... | collective-permute-start | bytes 49160 | tf_op jit(solution)/shard_map/ppermute | solution.py:153
  207.1 3.0 %copy-start = (bf16[1,16,32768]{2,1,0:T(8,128)(2,1)S(1)}, bf16[1,16,32768]{2,1,0:T(8,128)(2,1)}, u32[]{:S(2)}) copy-start(bf16[1,16,32768]{2,1,0:T(8,128)(2,1)} %param.13) | copy-start | bytes 3145732

commit v4 on v3

--- a/solution.py
+++ b/solution.py
@@ -82,7 +82,7 @@
 
     def kernel(index_ref, field_ref, out_ref):
         def body(i, carry):
-            row = jnp.clip(index_ref[i], 0, field_rows - 1)
+            row = index_ref[i]
             out_ref[pl.ds(i, 1), :] = field_ref[pl.ds(row, 1), :]
             return carry
 
@@ -101,23 +101,25 @@
     )(index, field)
 
 
-def scatter_regions(index, update, region_rows, splits):
+def scatter_regions(index, lane, value, region_rows, splits):
     regions = len(region_rows)
     per_region = index.shape[0] // regions
     per_stream = per_region // splits
     total_rows = sum(region_rows)
 
-    def kernel(index_ref, update_ref, out_ref, *accs):
+    def kernel(index_ref, lane_ref, value_ref, out_ref, *accs):
         for acc in accs:
             acc[...] = jnp.zeros_like(acc)
+        lanes = lax.broadcasted_iota(jnp.int32, (1, LANES), 1)
 
         def body(j, carry):
             for region in range(regions):
                 for split in range(splits):
                     i = region * per_region + split * per_stream + j
-                    row = jnp.clip(index_ref[i], 0, region_rows[region])
+                    row = index_ref[i]
+                    hit = jnp.where(lanes == lane_ref[i], value_ref[i], 0.0)
                     acc = accs[region * splits + split]
-                    acc[pl.ds(row, 1), :] += update_ref[pl.ds(i, 1), :]
+                    acc[pl.ds(row, 1), :] += hit
             return carry
 
         lax.fori_loop(0, per_stream, body, 0, unroll=2)
@@ -134,10 +136,10 @@
         kernel,
         out_shape=jax.ShapeDtypeStruct((total_rows, LANES), jnp.bfloat16),
         grid_spec=pltpu.PrefetchScalarGridSpec(
-            num_scalar_prefetch=1,
+            num_scalar_prefetch=3,
             grid=(1,),
-            in_specs=[pl.BlockSpec(update.shape, lambda i, index: (0, 0))],
-            out_specs=pl.BlockSpec((total_rows, LANES), lambda i, index: (0, 0)),
+            in_specs=[],
+            out_specs=pl.BlockSpec((total_rows, LANES), lambda i, *refs: (0, 0)),
             scratch_shapes=[
                 pltpu.VMEM((rows + 8, LANES), jnp.float32)
                 for rows in region_rows
@@ -145,7 +147,7 @@
             ],
         ),
         compiler_params=pltpu.CompilerParams(vmem_limit_bytes=48 * 1024 * 1024),
-    )(index, update)
+    )(index, lane, value)
 
 
 def neighbours(value, axis):
@@ -165,7 +167,7 @@
     padded = padded_2(y_smooth, (("gx", 1),), tap_reach)
     smoothed = along_x(padded, slab_rows)
 
-    obs_row = obs_cell // LANES
+    obs_row = jnp.clip(obs_cell // LANES, 0, rows - 1)
     lane_hit = lax.broadcasted_iota(jnp.int32, (nobs, LANES), 1) == (obs_cell % LANES)[:, None]
     s_rows = gather_rows(obs_row, smoothed.reshape(rows, LANES))
     s_val = jnp.sum(jnp.where(lane_hit, s_rows, 0.0), axis=1)
@@ -179,7 +181,8 @@
 
     plane_rows = plane_cells // LANES
     halo_rows = tap_reach * plane_rows
-    left_cell, right_cell = neighbours(obs_cell, "gx")
+    late_cell, contrib = lax.optimization_barrier((obs_cell, contrib))
+    left_cell, right_cell = neighbours(late_cell, "gx")
     left_contrib, right_contrib = neighbours(contrib, "gx")
     left_row = jnp.where(
         left_cell >= (slab_rows - tap_reach) * plane_cells,
@@ -188,11 +191,13 @@
     )
     right_row = jnp.where(right_cell < tap_reach * plane_cells, right_cell // LANES, halo_rows)
     all_cell = jnp.concatenate([left_cell, obs_cell, right_cell])
-    all_row = jnp.concatenate([left_row, obs_row, right_row])
+    all_row = jnp.concatenate([
+        jnp.clip(left_row, 0, halo_rows), obs_row, jnp.clip(right_row, 0, halo_rows)
+    ])
     all_contrib = jnp.concatenate([left_contrib, contrib, right_contrib])
-    all_hit = lax.broadcasted_iota(jnp.int32, (3 * nobs, LANES), 1) == (all_cell % LANES)[:, None]
-    update = jnp.where(all_hit, all_contrib[:, None], 0.0)
-    extended = scatter_regions(all_row, update, (halo_rows, rows, halo_rows), 2)
+    extended = scatter_regions(
+        all_row, all_cell % LANES, all_contrib, (halo_rows, rows, halo_rows), 2
+    )
     padded_back = extended.reshape(members, slab_rows + 2 * tap_reach, plane_cells)
     x_back = along_x(padded_back, slab_rows).astype(jnp.bfloat16)
     y_back = along_y(x_back).astype(jnp.bfloat16)

time: 212 us -> 179 us (0.84)
  the two profiles are of different devices: /device:TPU:6 before, /device:TPU:480 now
where the time goes in v4:
time: 179 us
  waiting for transfers between devices  54.8 us (31%)
  starting transfers between devices  35.6 us (20%)
  local copies, waits for them, and re-layouts  35.5 us (20%)
  Pallas kernels  35 us (20%)
  matrix products  13.6 us (8%)
  other arithmetic  3.2 us (2%)
    pallas_call x1, Pallas kernels, scatter_regions(): pl.pallas_call(kernel, out_shape=jax.ShapeDtypeStruct((total_rows, LANES)...  29 us
    ppermute x1, waiting for transfers between devices, padded_2(): lax.ppermute(lax.slice_in_dim(block, 0, width, axis=dim), axis, backward)  22.8 us
    ppermute x4, waiting for transfers between devices, butterfly_sum(): partner = lax.ppermute(value, axis, [(i, i ^ step) for i in range(count)])  17.1 us
    gather x1, local copies, waits for them, and re-layouts, local(): perturbations.reshape(slot_count * rows, LANES)[obs_slot * rows + obs_row]  15 us
    ppermute x4, starting transfers between devices, butterfly_sum(): partner = lax.ppermute(value, axis, [(i, i ^ step) for i in range(count)])  12.4 us
    ppermute x2, waiting for transfers between devices, neighbours(): lax.ppermute(value, axis, [(i + 1, i) for i in range(count - 1)])  11 us
    ppermute x2, starting transfers between devices, neighbours(): lax.ppermute(value, axis, [(i, i + 1) for i in range(count - 1)])  8.52 us
    ppermute x1, starting transfers between devices, padded_2(): lax.ppermute(lax.slice_in_dim(block, block.shape[dim] - width, None, axis...  7.71 us
  transfers between devices with their start and end apart: 10, of which 7 were waited for; matrix products, arithmetic and copies ran while one was open for 10% of the time, Pallas kernels for 0%

profile of v4, /device:TPU:480, one launch (start us, length us, event | category | flops | bytes accessed | tf_op | source)
XLA Modules:
  0.0 178.6 jit_solution(120541569969012186)
XLA Ops:
  0.0 3.0 %reshape.69 = bf16[16,512,64]{2,1,0:T(8,128)(2,1)S(1)} reshape(bf16[1,16,32768]{2,1,0:T(8,128)(2,1)} %param.13) | data formatting | bytes 2097152 | tf_op jit(solution)/shard_map/reshape
  3.1 0.0 copy-done.2
  3.1 2.5 %fusion.7 = bf16[1,16,512,64]{2,3,1,0:T(8,128)(2,1)S(1)} fusion(bf16[512,512,1]{1,0,2:T(8,128)(2,1)} %constant.83, bf16[64,64,1]{1,0,2:T(8,128)(2,1)S(1)} %copy-done.2, bf16[16,512,64]{2,1,0:T(8,128)(2,1)S(1)} %reshape.69), kind=kOutput, calls=%fused_computation.18 | convolution fusion | flops 605028352 | bytes 2629632 | tf_op jit(solution)/shard_map/mxqz,yq->mxyz/dot_general | solution.py:60
  5.6 1.1 copy.15
  6.6 1.7 convert_element_type.68
  8.3 1.5 fusion.24
  9.9 7.7 %collective-permute-start = (bf16[1,15,32768]{2,1,0:T(8,128)(2,1)}, bf16[1,15,32768]{2,1,0:T(8,128)(2,1)}, u32[]{:S(2)}, u32[]{:S(2)}) collective-permute-start(bf16[1,15,32768]{2,1,0:T(8,128)(2,1)} %get-tuple-element.11), channel_id=1, source_target_pairs={{0,1},{1,2},{2,3},{3,4},{4,5},{5,6},{6,7},{7,8},{8,9},{9,10},{10,1... | collective-permute-start | bytes 2949128 | tf_op jit(solution)/shard_map/ppermute | solution.py:23
  17.6 0.0 copy-start.3
  17.6 0.0 copy-start.4
  17.6 1.9 %collective-permute-start.1 = (bf16[1,15,32768]{2,1,0:T(8,128)(2,1)}, bf16[1,15,32768]{2,1,0:T(8,128)(2,1)}, u32[]{:S(2)}, u32[]{:S(2)}) collective-permute-start(bf16[1,15,32768]{2,1,0:T(8,128)(2,1)} %get-tuple-element.12), channel_id=1, source_target_pairs={{1,0},{2,1},{3,2},{4,3},{5,4},{6,5},{7,6},{8,7},{9,8},{10,9},{11,1... | collective-permute-start | bytes 2949128 | tf_op jit(solution)/shard_map/ppermute | solution.py:26
  19.6 2.9 %reshape.68 = bf16[8192,128]{1,0:T(8,128)(2,1)S(1)} reshape(bf16[2,1,16,32768]{3,2,1,0:T(8,128)(2,1)} %param.14) | data formatting | bytes 4194304 | tf_op jit(solution)/shard_map/reshape | solution.py:174
  22.4 0.0 copy-done.3
  22.5 0.0 copy-done.4
  22.5 0.0 copy-start.7
  22.5 15.0 %gather_fusion = bf16[4096,128]{1,0:T(8,128)(2,1)} fusion(bf16[8192,128]{1,0:T(8,128)(2,1)S(1)} %reshape.68, s32[4096]{0:T(1024)S(1)} %get-tuple-element.17), kind=kCustom, calls=%fused_computation | custom fusion | bytes 2113536 | tf_op jit(solution)/shard_map/gather | solution.py:174
  37.5 3.9 %collective-permute-done = bf16[1,15,32768]{2,1,0:T(8,128)(2,1)} collective-permute-done((bf16[1,15,32768]{2,1,0:T(8,128)(2,1)}, bf16[1,15,32768]{2,1,0:T(8,128)(2,1)}, u32[]{:S(2)}, u32[]{:S(2)}) %collective-permute-start) | collective-permute-done | bytes 983072 | tf_op jit(solution)/shard_map/ppermute | solution.py:23
  41.4 22.8 %collective-permute-done.1 = bf16[1,15,32768]{2,1,0:T(8,128)(2,1)} collective-permute-done((bf16[1,15,32768]{2,1,0:T(8,128)(2,1)}, bf16[1,15,32768]{2,1,0:T(8,128)(2,1)}, u32[]{:S(2)}, u32[]{:S(2)}) %collective-permute-start.1) | collective-permute-done | bytes 983072 | tf_op jit(solution)/shard_map/ppermute | solution.py:26
  64.3 0.0 copy-done.7
  64.3 3.8 %convolution_bitcast_fusion = f32[1,16,32768]{2,1,0:T(8,128)} fusion(bf16[16,46]{1,0:T(8,128)(2,1)S(1)} %copy-done.7, bf16[1,15,32768]{2,1,0:T(8,128)(2,1)} %collective-permute-done.1, bf16[1,16,32768]{2,1,0:T(8,128)(2,1)S(1)} %convert_element_type.68, bf16[1,15,32768]{2,1,0:T(8,128)(2,1)} %collective-permute-done), kind=kOutput, calls=%fused_computation.1 | convolution fusion | flops 57278464 | bytes 5113280 | tf_op jit(solution)/shard_map/ip,mpc->mic/dot_general | solution.py:66
  68.1 1.7 reshape.71.field_ref
  69.8 5.9 %shard_map.127 = f32[4096,128]{1,0:T(8,128)S(1)} custom-call(s32[4096]{0:T(1024)S(1)} %get-tuple-element.18.index_ref, f32[4096,128]{1,0:T(8,128)S(1)} %reshape.71.field_ref), custom_call_target="tpu_custom_call" | custom-call | tf_op jit(solution)/shard_map/pallas_call | solution.py:91
  75.8 0.0 copy-start.5
  75.8 0.0 copy-start.6
  75.8 1.6 select_reduce_fusion
  77.4 1.9 %collective-permute-start.2 = (f32[4096]{0:T(1024)S(1)}, f32[4096]{0:T(1024)S(1)}, u32[]{:S(2)}, u32[]{:S(2)}) collective-permute-start(f32[4096]{0:T(1024)S(1)} %mul.21), channel_id=1, source_target_pairs={{0,32},{32,0},{64,96},{96,64},{128,160},{160,128},{192,224},{224,1... | collective-permute-start | bytes 49160 | tf_op jit(solution)/shard_map/ppermute | solution.py:73
  79.3 1.1 collective-permute-done.2
  80.5 3.5 %collective-permute-start.3 = (f32[4096]{0:T(1024)S(1)}, f32[4096]{0:T(1024)S(1)}, u32[]{:S(2)}, u32[]{:S(2)}) collective-permute-start(f32[4096]{0:T(1024)S(1)} %add.44), channel_id=1, source_target_pairs={{0,64},{32,96},{64,0},{96,32},{128,192},{160,224},{192,128},{224,1... | collective-permute-start | bytes 49160 | tf_op jit(solution)/shard_map/ppermute | solution.py:73
  83.9 2.1 %collective-permute-done.3 = f32[4096]{0:T(1024)S(1)} collective-permute-done((f32[4096]{0:T(1024)S(1)}, f32[4096]{0:T(1024)S(1)}, u32[]{:S(2)}, u32[]{:S(2)}) %collective-permute-start.3) | collective-permute-done | bytes 16416 | tf_op jit(solution)/shard_map/ppermute | solution.py:73
  86.1 5.1 %collective-permute-start.4 = (f32[4096]{0:T(1024)S(1)}, f32[4096]{0:T(1024)S(1)}, u32[]{:S(2)}, u32[]{:S(2)}) collective-permute-start(f32[4096]{0:T(1024)S(1)} %add.45), channel_id=1, source_target_pairs={{0,128},{32,160},{64,192},{96,224},{128,0},{160,32},{192,64},{224,... | collective-permute-start | bytes 49160 | tf_op jit(solution)/shard_map/ppermute | solution.py:73
  91.2 2.0 %collective-permute-done.4 = f32[4096]{0:T(1024)S(1)} collective-permute-done((f32[4096]{0:T(1024)S(1)}, f32[4096]{0:T(1024)S(1)}, u32[]{:S(2)}, u32[]{:S(2)}) %collective-permute-start.4) | collective-permute-done | bytes 16416 | tf_op jit(solution)/shard_map/ppermute | solution.py:73
  93.2 1.9 %collective-permute-start.5 = (f32[4096]{0:T(1024)S(1)}, f32[4096]{0:T(1024)S(1)}, u32[]{:S(2)}, u32[]{:S(2)}) collective-permute-start(f32[4096]{0:T(1024)S(1)} %add.46), channel_id=1, source_target_pairs={{0,256},{32,288},{64,320},{96,352},{128,384},{160,416},{192,448},{... | collective-permute-start | bytes 49160 | tf_op jit(solution)/shard_map/ppermute | solution.py:73
  95.8 11.8 %collective-permute-done.5 = f32[4096]{0:T(1024)S(1)} collective-permute-done((f32[4096]{0:T(1024)S(1)}, f32[4096]{0:T(1024)S(1)}, u32[]{:S(2)}, u32[]{:S(2)}) %collective-permute-start.5) | collective-permute-done | bytes 16416 | tf_op jit(solution)/shard_map/ppermute | solution.py:73
  107.6 0.0 copy-done.5
  107.6 5.6 %collective-permute-start.6 = (s32[4096]{0:T(1024)S(1)}, s32[4096]{0:T(1024)S(1)}, u32[]{:S(2)}, u32[]{:S(2)}) collective-permute-start(s32[4096]{0:T(1024)S(1)} %copy-done.3), channel_id=1, source_target_pairs={{0,1},{1,2},{2,3},{3,4},{4,5},{5,6},{6,7},{7,8},{8,9},{9,10},{10,1... | collective-permute-start | bytes 49160 | tf_op jit(solution)/shard_map/ppermute | solution.py:155
  113.2 2.9 %collective-permute-start.8 = (f32[4096]{0:T(1024)S(1)}, f32[4096]{0:T(1024)S(1)}, u32[]{:S(2)}, u32[]{:S(2)}) collective-permute-start(f32[4096]{0:T(1024)S(1)} %multiply_multiply_fusion), channel_id=1, source_target_pairs={{0,1},{1,2},{2,3},{3,4},{4,5},{5,6},{6,7},{7,8},{8,9},{9,10},{10,1... | collective-permute-start | bytes 49160 | tf_op jit(solution)/shard_map/ppermute | solution.py:155
  116.1 2.9 %collective-permute-start.9 = (f32[4096]{0:T(1024)S(1)}, f32[4096]{0:T(1024)S(1)}, u32[]{:S(2)}, u32[]{:S(2)}) collective-permute-start(f32[4096]{0:T(1024)S(1)} %multiply_multiply_fusion), channel_id=1, source_target_pairs={{1,0},{2,1},{3,2},{4,3},{5,4},{6,5},{7,6},{8,7},{9,8},{10,9},{11,1... | collective-permute-start | bytes 49160 | tf_op jit(solution)/shard_map/ppermute | solution.py:156
  119.0 2.1 %collective-permute-start.7 = (s32[4096]{0:T(1024)S(1)}, s32[4096]{0:T(1024)S(1)}, u32[]{:S(2)}, u32[]{:S(2)}) collective-permute-start(s32[4096]{0:T(1024)S(1)} %copy-done.3), channel_id=1, source_target_pairs={{1,0},{2,1},{3,2},{4,3},{5,4},{6,5},{7,6},{8,7},{9,8},{10,9},{11,1... | collective-permute-start | bytes 49160 | tf_op jit(solution)/shard_map/ppermute | solution.py:156
  121.2 0.0 collective-permute-done.6
  121.2 11.0 %collective-permute-done.7 = s32[4096]{0:T(1024)S(1)} collective-permute-done((s32[4096]{0:T(1024)S(1)}, s32[4096]{0:T(1024)S(1)}, u32[]{:S(2)}, u32[]{:S(2)}) %collective-permute-start.7) | collective-permute-done | bytes 16416 | tf_op jit(solution)/shard_map/ppermute | solution.py:156
  132.2 0.0 collective-permute-done.8
  132.2 0.0 collective-permute-done.9
  132.3 29.0 %shard_map.128 = bf16[11776,128]{1,0:T(8,128)(2,1)S(1)} custom-call(s32[12288]{0:T(1024)S(1)} %get-tuple-element.21.index_ref, s32[12288]{0:T(1024)S(1)} %get-tuple-element.20.lane_ref, f32[12288]{0:T(1024)S(1)} %pad_maximum_fusion.value_ref), custom_call_target="tpu_custom_call" | custom-call | tf_op jit(solution)/shard_map/pallas_call | solution.py:135
  161.3 3.2 %reshape.72 = bf16[46,32768]{1,0:T(8,128)(2,1)} reshape(bf16[11776,128]{1,0:T(8,128)(2,1)S(1)} %shard_map.128) | data formatting | bytes 6029312 | tf_op jit(solution)/shard_map/reshape.7
  164.5 2.4 %fusion = bf16[1,16,32768]{2,1,0:T(8,128)(2,1)S(1)} fusion(bf16[46,32768]{1,0:T(8,128)(2,1)} %reshape.72, bf16[16,46]{1,0:T(8,128)(2,1)S(1)} %copy-done.7), kind=kOutput, calls=%fused_computation.3 | convolution fusion | flops 48758784 | bytes 4064704 | tf_op jit(solution)/shard_map/ip,mpc->mic/dot_general | solution.py:66
  166.9 2.3 %reshape.73 = bf16[16,512,64]{2,1,0:T(8,128)(2,1)S(1)} reshape(bf16[1,16,32768]{2,1,0:T(8,128)(2,1)S(1)} %fusion) | data formatting | bytes 2097152 | tf_op jit(solution)/shard_map/reshape.9
  169.2 4.9 %fusion.8 = f32[16,512,64]{2,1,0:T(8,128)} fusion(bf16[64,64,1]{1,0,2:T(8,128)(2,1)S(1)} %copy-done.2, bf16[16,512,64]{2,1,0:T(8,128)(2,1)S(1)} %reshape.73, bf16[512,512,1]{1,0,2:T(8,128)(2,1)} %constant.83), kind=kOutput, calls=%fused_computation.19 | convolution fusion | flops 604504064 | bytes 3678208 | tf_op jit(solution)/shard_map/mxyq,zq->mxyz/dot_general | solution.py:52
  174.1 3.0 %reshape.75 = f32[1,16,32768]{2,1,0:T(8,128)S(1)} reshape(f32[16,512,64]{2,1,0:T(8,128)} %fusion.8) | data formatting | bytes 4194304 | tf_op jit(solution)/shard_map/reshape | solution.py:53
  177.1 1.5 convert_add_fusion
  (17 shorter events, 0.1 us)
Async XLA Ops:
  0.0 3.1 %copy-start.2 = (bf16[64,64,1]{1,0,2:T(8,128)(2,1)S(1)}, bf16[64,64,1]{1,0,2:T(8,128)(2,1)}, u32[]{:S(2)}) copy-start(bf16[64,64,1]{1,0,2:T(8,128)(2,1)} %constant.82) | copy-start | bytes 24580
  9.9 31.6 %collective-permute-start = (bf16[1,15,32768]{2,1,0:T(8,128)(2,1)}, bf16[1,15,32768]{2,1,0:T(8,128)(2,1)}, u32[]{:S(2)}, u32[]{:S(2)}) collective-permute-start(bf16[1,15,32768]{2,1,0:T(8,128)(2,1)} %get-tuple-element.11), channel_id=1, source_target_pairs={{0,1},{1,2},{2,3},{3,4},{4,5},{5,6},{6,7},{7,8},{8,9},{9,10},{10,1... | collective-permute-start | bytes 2949128 | tf_op jit(solution)/shard_map/ppermute | solution.py:23
  17.6 4.8 %copy-start.3 = (s32[4096]{0:T(1024)S(1)}, s32[4096]{0:T(1024)}, u32[]{:S(2)}) copy-start(s32[4096]{0:T(1024)} %param.15) | copy-start | bytes 49156
  17.6 4.8 %copy-start.4 = (s32[4096]{0:T(1024)S(1)}, s32[4096]{0:T(1024)}, u32[]{:S(2)}) copy-start(s32[4096]{0:T(1024)} %param.16) | copy-start | bytes 49156
  17.6 46.6 %collective-permute-start.1 = (bf16[1,15,32768]{2,1,0:T(8,128)(2,1)}, bf16[1,15,32768]{2,1,0:T(8,128)(2,1)}, u32[]{:S(2)}, u32[]{:S(2)}) collective-permute-start(bf16[1,15,32768]{2,1,0:T(8,128)(2,1)} %get-tuple-element.12), channel_id=1, source_target_pairs={{1,0},{2,1},{3,2},{4,3},{5,4},{6,5},{7,6},{8,7},{9,8},{10,9},{11,1... | collective-permute-start | bytes 2949128 | tf_op jit(solution)/shard_map/ppermute | solution.py:26
  22.5 41.8 %copy-start.7 = (bf16[16,46]{1,0:T(8,128)(2,1)S(1)}, bf16[16,46]{1,0:T(8,128)(2,1)}, u32[]{:S(2)}) copy-start(bf16[16,46]{1,0:T(8,128)(2,1)} %constant.78.clone) | copy-start | bytes 4420
  69.8 6.0 %copy-start.1 = (bf16[4096,128]{1,0:T(8,128)(2,1)S(1)}, bf16[4096,128]{1,0:T(8,128)(2,1)}, u32[]{:S(2)}) copy-start(bf16[4096,128]{1,0:T(8,128)(2,1)} %gather_fusion) | copy-start | bytes 3145732
  75.8 31.8 %copy-start.5 = (f32[4096]{0:T(1024)S(1)}, f32[4096]{0:T(1024)}, u32[]{:S(2)}) copy-start(f32[4096]{0:T(1024)} %param.17) | copy-start | bytes 49156
  75.8 31.8 %copy-start.6 = (f32[4096]{0:T(1024)S(1)}, f32[4096]{0:T(1024)}, u32[]{:S(2)}) copy-start(f32[4096]{0:T(1024)} %param.18) | copy-start | bytes 49156
  77.4 3.1 %collective-permute-start.2 = (f32[4096]{0:T(1024)S(1)}, f32[4096]{0:T(1024)S(1)}, u32[]{:S(2)}, u32[]{:S(2)}) collective-permute-start(f32[4096]{0:T(1024)S(1)} %mul.21), channel_id=1, source_target_pairs={{0,32},{32,0},{64,96},{96,64},{128,160},{160,128},{192,224},{224,1... | collective-permute-start | bytes 49160 | tf_op jit(solution)/shard_map/ppermute | solution.py:73
  80.5 5.6 %collective-permute-start.3 = (f32[4096]{0:T(1024)S(1)}, f32[4096]{0:T(1024)S(1)}, u32[]{:S(2)}, u32[]{:S(2)}) collective-permute-start(f32[4096]{0:T(1024)S(1)} %add.44), channel_id=1, source_target_pairs={{0,64},{32,96},{64,0},{96,32},{128,192},{160,224},{192,128},{224,1... | collective-permute-start | bytes 49160 | tf_op jit(solution)/shard_map/ppermute | solution.py:73
  86.1 7.1 %collective-permute-start.4 = (f32[4096]{0:T(1024)S(1)}, f32[4096]{0:T(1024)S(1)}, u32[]{:S(2)}, u32[]{:S(2)}) collective-permute-start(f32[4096]{0:T(1024)S(1)} %add.45), channel_id=1, source_target_pairs={{0,128},{32,160},{64,192},{96,224},{128,0},{160,32},{192,64},{224,... | collective-permute-start | bytes 49160 | tf_op jit(solution)/shard_map/ppermute | solution.py:73
  93.2 14.3 %collective-permute-start.5 = (f32[4096]{0:T(1024)S(1)}, f32[4096]{0:T(1024)S(1)}, u32[]{:S(2)}, u32[]{:S(2)}) collective-permute-start(f32[4096]{0:T(1024)S(1)} %add.46), channel_id=1, source_target_pairs={{0,256},{32,288},{64,320},{96,352},{128,384},{160,416},{192,448},{... | collective-permute-start | bytes 49160 | tf_op jit(solution)/shard_map/ppermute | solution.py:73
  107.6 13.6 %collective-permute-start.6 = (s32[4096]{0:T(1024)S(1)}, s32[4096]{0:T(1024)S(1)}, u32[]{:S(2)}, u32[]{:S(2)}) collective-permute-start(s32[4096]{0:T(1024)S(1)} %copy-done.3), channel_id=1, source_target_pairs={{0,1},{1,2},{2,3},{3,4},{4,5},{5,6},{6,7},{7,8},{8,9},{9,10},{10,1... | collective-permute-start | bytes 49160 | tf_op jit(solution)/shard_map/ppermute | solution.py:155
  113.2 19.1 %collective-permute-start.8 = (f32[4096]{0:T(1024)S(1)}, f32[4096]{0:T(1024)S(1)}, u32[]{:S(2)}, u32[]{:S(2)}) collective-permute-start(f32[4096]{0:T(1024)S(1)} %multiply_multiply_fusion), channel_id=1, source_target_pairs={{0,1},{1,2},{2,3},{3,4},{4,5},{5,6},{6,7},{7,8},{8,9},{9,10},{10,1... | collective-permute-start | bytes 49160 | tf_op jit(solution)/shard_map/ppermute | solution.py:155
  116.1 16.1 %collective-permute-start.9 = (f32[4096]{0:T(1024)S(1)}, f32[4096]{0:T(1024)S(1)}, u32[]{:S(2)}, u32[]{:S(2)}) collective-permute-start(f32[4096]{0:T(1024)S(1)} %multiply_multiply_fusion), channel_id=1, source_target_pairs={{1,0},{2,1},{3,2},{4,3},{5,4},{6,5},{7,6},{8,7},{9,8},{10,9},{11,1... | collective-permute-start | bytes 49160 | tf_op jit(solution)/shard_map/ppermute | solution.py:156
  119.0 13.1 %collective-permute-start.7 = (s32[4096]{0:T(1024)S(1)}, s32[4096]{0:T(1024)S(1)}, u32[]{:S(2)}, u32[]{:S(2)}) collective-permute-start(s32[4096]{0:T(1024)S(1)} %copy-done.3), channel_id=1, source_target_pairs={{1,0},{2,1},{3,2},{4,3},{5,4},{6,5},{7,6},{8,7},{9,8},{10,9},{11,1... | collective-permute-start | bytes 49160 | tf_op jit(solution)/shard_map/ppermute | solution.py:156
  174.1 3.0 %copy-start = (bf16[1,16,32768]{2,1,0:T(8,128)(2,1)S(1)}, bf16[1,16,32768]{2,1,0:T(8,128)(2,1)}, u32[]{:S(2)}) copy-start(bf16[1,16,32768]{2,1,0:T(8,128)(2,1)} %param.13) | copy-start | bytes 3145732

commit v5 on v4

--- a/solution.py
+++ b/solution.py
@@ -66,14 +66,27 @@
     return jnp.einsum("ip,mpc->mic", band_x, padded, preferred_element_type=jnp.float32)
 
 
+def group_sum(value, axis, bits):
+    count = lax.axis_size(axis)
+    codes = [0]
+    for bit in bits:
+        codes = codes + [code | (1 << bit) for code in codes]
+    received = {0: value}
+    for code in codes[1:]:
+        received[code] = lax.ppermute(value, axis, [(i, i ^ code) for i in range(count)])
+    own = lax.axis_index(axis) & sum(1 << bit for bit in bits)
+    total = None
+    for code in codes:
+        term = received[code]
+        for mine in codes[1:]:
+            term = jnp.where(own == mine, received[code ^ mine], term)
+        total = term if total is None else total + term
+    return total
+
+
 def butterfly_sum(value, axis):
-    count = lax.axis_size(axis)
-    step = 1
-    while step < count:
-        partner = lax.ppermute(value, axis, [(i, i ^ step) for i in range(count)])
-        value = value + partner
-        step *= 2
-    return value
+    value = group_sum(value, axis, (0, 1))
+    return group_sum(value, axis, (2, 3))
 
 
 def gather_rows(index, field):

time: 179 us -> 186 us (1.039)
  the two profiles are of different devices: /device:TPU:480 before, /device:TPU:2 now
where the time goes in v5:
time: 186 us; the launch traced here: 185 us
  starting transfers between devices  63.6 us (34%)
  local copies, waits for them, and re-layouts  35.5 us (19%)
  Pallas kernels  35 us (19%)
  waiting for transfers between devices  32.9 us (18%)
  matrix products  13.6 us (7%)
  other arithmetic  3.21 us (2%)
    ppermute x6, starting transfers between devices, group_sum(): lax.ppermute(value, axis, [(i, i ^ code) for i in range(count)])  29.2 us
    pallas_call x1, Pallas kernels, scatter_regions(): pl.pallas_call(kernel, out_shape=jax.ShapeDtypeStruct((total_rows, LANES)...  29 us
    ppermute x1, waiting for transfers between devices, padded_2(): lax.ppermute(lax.slice_in_dim(block, 0, width, axis=dim), axis, backward)  15.8 us
    gather x1, local copies, waits for them, and re-layouts, local(): perturbations.reshape(slot_count * rows, LANES)[obs_slot * rows + obs_row]  15 us
    ppermute x2, starting transfers between devices, neighbours(): lax.ppermute(value, axis, [(i + 1, i) for i in range(count - 1)])  13.4 us
    ppermute x1, starting transfers between devices, padded_2(): lax.ppermute(lax.slice_in_dim(block, 0, width, axis=dim), axis, backward)  11.2 us
    ppermute x6, waiting for transfers between devices, group_sum(): lax.ppermute(value, axis, [(i, i ^ code) for i in range(count)])  10.1 us
    dot_general x2, matrix products, along_x(): jnp.einsum('ip,mpc->mic', band_x, padded, preferred_element_type=jnp.floa...  6.24 us
  transfers between devices with their start and end apart: 12, of which 5 were waited for; matrix products, arithmetic and copies ran while one was open for 10% of the time, Pallas kernels for 0%

profile of v5, /device:TPU:2, one launch (start us, length us, event | category | flops | bytes accessed | tf_op | source)
XLA Modules:
  0.0 184.8 jit_solution(4630012732255141333)
XLA Ops:
  0.0 3.0 %reshape.69 = bf16[16,512,64]{2,1,0:T(8,128)(2,1)S(1)} reshape(bf16[1,16,32768]{2,1,0:T(8,128)(2,1)} %param.13) | data formatting | bytes 2097152 | tf_op jit(solution)/shard_map/reshape
  3.1 0.0 copy-done.2
  3.1 2.5 %fusion.7 = bf16[1,16,512,64]{2,3,1,0:T(8,128)(2,1)S(1)} fusion(bf16[512,512,1]{1,0,2:T(8,128)(2,1)} %constant.100, bf16[64,64,1]{1,0,2:T(8,128)(2,1)S(1)} %copy-done.2, bf16[16,512,64]{2,1,0:T(8,128)(2,1)S(1)} %reshape.69), kind=kOutput, calls=%fused_computation.18 | convolution fusion | flops 605028352 | bytes 2629632 | tf_op jit(solution)/shard_map/mxqz,yq->mxyz/dot_general | solution.py:60
  5.6 1.1 copy.15
  6.6 1.7 convert_element_type.68
  8.3 1.5 fusion.24
  9.9 3.8 %collective-permute-start = (bf16[1,15,32768]{2,1,0:T(8,128)(2,1)}, bf16[1,15,32768]{2,1,0:T(8,128)(2,1)}, u32[]{:S(2)}, u32[]{:S(2)}) collective-permute-start(bf16[1,15,32768]{2,1,0:T(8,128)(2,1)} %get-tuple-element.11), channel_id=1, source_target_pairs={{0,1},{1,2},{2,3},{3,4},{4,5},{5,6},{6,7},{7,8},{8,9},{9,10},{10,1... | collective-permute-start | bytes 2949128 | tf_op jit(solution)/shard_map/ppermute | solution.py:23
  13.7 0.0 copy-start.3
  13.7 0.0 copy-start.4
  13.7 11.2 %collective-permute-start.1 = (bf16[1,15,32768]{2,1,0:T(8,128)(2,1)}, bf16[1,15,32768]{2,1,0:T(8,128)(2,1)}, u32[]{:S(2)}, u32[]{:S(2)}) collective-permute-start(bf16[1,15,32768]{2,1,0:T(8,128)(2,1)} %get-tuple-element.12), channel_id=1, source_target_pairs={{1,0},{2,1},{3,2},{4,3},{5,4},{6,5},{7,6},{8,7},{9,8},{10,9},{11,1... | collective-permute-start | bytes 2949128 | tf_op jit(solution)/shard_map/ppermute | solution.py:26
  25.0 2.9 %reshape.68 = bf16[8192,128]{1,0:T(8,128)(2,1)S(1)} reshape(bf16[2,1,16,32768]{3,2,1,0:T(8,128)(2,1)} %param.14) | data formatting | bytes 4194304 | tf_op jit(solution)/shard_map/reshape | solution.py:187
  27.9 0.0 copy-start.7
  27.9 15.0 %gather_fusion = bf16[4096,128]{1,0:T(8,128)(2,1)} fusion(bf16[8192,128]{1,0:T(8,128)(2,1)S(1)} %reshape.68, s32[4096]{0:T(1024)S(1)} %get-tuple-element.17), kind=kCustom, calls=%fused_computation | custom fusion | bytes 2113536 | tf_op jit(solution)/shard_map/gather | solution.py:187
  43.0 4.4 %collective-permute-done = bf16[1,15,32768]{2,1,0:T(8,128)(2,1)} collective-permute-done((bf16[1,15,32768]{2,1,0:T(8,128)(2,1)}, bf16[1,15,32768]{2,1,0:T(8,128)(2,1)}, u32[]{:S(2)}, u32[]{:S(2)}) %collective-permute-start) | collective-permute-done | bytes 983072 | tf_op jit(solution)/shard_map/ppermute | solution.py:23
  47.4 15.8 %collective-permute-done.1 = bf16[1,15,32768]{2,1,0:T(8,128)(2,1)} collective-permute-done((bf16[1,15,32768]{2,1,0:T(8,128)(2,1)}, bf16[1,15,32768]{2,1,0:T(8,128)(2,1)}, u32[]{:S(2)}, u32[]{:S(2)}) %collective-permute-start.1) | collective-permute-done | bytes 983072 | tf_op jit(solution)/shard_map/ppermute | solution.py:26
  63.2 3.8 %convolution_bitcast_fusion = f32[1,16,32768]{2,1,0:T(8,128)} fusion(bf16[16,46]{1,0:T(8,128)(2,1)S(1)} %copy-done.7, bf16[1,15,32768]{2,1,0:T(8,128)(2,1)} %collective-permute-done.1, bf16[1,16,32768]{2,1,0:T(8,128)(2,1)S(1)} %convert_element_type.68, bf16[1,15,32768]{2,1,0:T(8,128)(2,1)} %collective-permute-done), kind=kOutput, calls=%fused_computation.1 | convolution fusion | flops 57278464 | bytes 5113280 | tf_op jit(solution)/shard_map/ip,mpc->mic/dot_general | solution.py:66
  67.1 1.7 reshape.71.field_ref
  68.8 5.9 %shard_map.127 = f32[4096,128]{1,0:T(8,128)S(1)} custom-call(s32[4096]{0:T(1024)S(1)} %get-tuple-element.18.index_ref, f32[4096,128]{1,0:T(8,128)S(1)} %reshape.71.field_ref), custom_call_target="tpu_custom_call" | custom-call | tf_op jit(solution)/shard_map/pallas_call | solution.py:104
  74.7 0.0 copy-start.5
  74.7 0.0 copy-start.6
  74.7 1.6 select_reduce_fusion
  76.4 2.0 %collective-permute-start.2 = (f32[4096]{0:T(1024)S(1)}, f32[4096]{0:T(1024)S(1)}, u32[]{:S(2)}, u32[]{:S(2)}) collective-permute-start(f32[4096]{0:T(1024)S(1)} %mul.21), channel_id=1, source_target_pairs={{0,96},{32,64},{64,32},{96,0},{128,224},{160,192},{192,160},{224,1... | collective-permute-start | bytes 49160 | tf_op jit(solution)/shard_map/ppermute | solution.py:76
  78.3 3.4 %collective-permute-start.3 = (f32[4096]{0:T(1024)S(1)}, f32[4096]{0:T(1024)S(1)}, u32[]{:S(2)}, u32[]{:S(2)}) collective-permute-start(f32[4096]{0:T(1024)S(1)} %mul.21), channel_id=1, source_target_pairs={{0,64},{32,96},{64,0},{96,32},{128,192},{160,224},{192,128},{224,1... | collective-permute-start | bytes 49160 | tf_op jit(solution)/shard_map/ppermute | solution.py:76
  81.8 2.2 %collective-permute-start.4 = (f32[4096]{0:T(1024)S(1)}, f32[4096]{0:T(1024)S(1)}, u32[]{:S(2)}, u32[]{:S(2)}) collective-permute-start(f32[4096]{0:T(1024)S(1)} %mul.21), channel_id=1, source_target_pairs={{0,32},{32,0},{64,96},{96,64},{128,160},{160,128},{192,224},{224,1... | collective-permute-start | bytes 49160 | tf_op jit(solution)/shard_map/ppermute | solution.py:76
  84.0 0.0 collective-permute-done.2
  84.0 0.0 collective-permute-done.3
  84.0 0.8 collective-permute-done.4
  84.9 17.2 %collective-permute-start.5 = (f32[4096]{0:T(1024)S(1)}, f32[4096]{0:T(1024)S(1)}, u32[]{:S(2)}, u32[]{:S(2)}) collective-permute-start(f32[4096]{0:T(1024)S(1)} %select_add_fusion), channel_id=1, source_target_pairs={{0,384},{32,416},{64,448},{96,480},{128,256},{160,288},{192,320},{... | collective-permute-start | bytes 49160 | tf_op jit(solution)/shard_map/ppermute | solution.py:76
  102.1 1.9 %collective-permute-start.6 = (f32[4096]{0:T(1024)S(1)}, f32[4096]{0:T(1024)S(1)}, u32[]{:S(2)}, u32[]{:S(2)}) collective-permute-start(f32[4096]{0:T(1024)S(1)} %select_add_fusion), channel_id=1, source_target_pairs={{0,256},{32,288},{64,320},{96,352},{128,384},{160,416},{192,448},{... | collective-permute-start | bytes 49160 | tf_op jit(solution)/shard_map/ppermute | solution.py:76
  104.0 2.5 %collective-permute-start.7 = (f32[4096]{0:T(1024)S(1)}, f32[4096]{0:T(1024)S(1)}, u32[]{:S(2)}, u32[]{:S(2)}) collective-permute-start(f32[4096]{0:T(1024)S(1)} %select_add_fusion), channel_id=1, source_target_pairs={{0,128},{32,160},{64,192},{96,224},{128,0},{160,32},{192,64},{224,... | collective-permute-start | bytes 49160 | tf_op jit(solution)/shard_map/ppermute | solution.py:76
  107.1 0.0 collective-permute-done.5
  107.1 9.3 %collective-permute-done.6 = f32[4096]{0:T(1024)S(1)} collective-permute-done((f32[4096]{0:T(1024)S(1)}, f32[4096]{0:T(1024)S(1)}, u32[]{:S(2)}, u32[]{:S(2)}) %collective-permute-start.6) | collective-permute-done | bytes 16416 | tf_op jit(solution)/shard_map/ppermute | solution.py:76
  116.4 0.0 collective-permute-done.7
  116.5 2.9 %collective-permute-start.8 = (s32[4096]{0:T(1024)S(1)}, s32[4096]{0:T(1024)S(1)}, u32[]{:S(2)}, u32[]{:S(2)}) collective-permute-start(s32[4096]{0:T(1024)S(1)} %copy-done.3), channel_id=1, source_target_pairs={{0,1},{1,2},{2,3},{3,4},{4,5},{5,6},{6,7},{7,8},{8,9},{9,10},{10,1... | collective-permute-start | bytes 49160 | tf_op jit(solution)/shard_map/ppermute | solution.py:168
  119.4 3.1 %collective-permute-start.10 = (f32[4096]{0:T(1024)S(1)}, f32[4096]{0:T(1024)S(1)}, u32[]{:S(2)}, u32[]{:S(2)}) collective-permute-start(f32[4096]{0:T(1024)S(1)} %multiply_multiply_fusion), channel_id=1, source_target_pairs={{0,1},{1,2},{2,3},{3,4},{4,5},{5,6},{6,7},{7,8},{8,9},{9,10},{10,1... | collective-permute-start | bytes 49160 | tf_op jit(solution)/shard_map/ppermute | solution.py:168
  122.5 10.3 %collective-permute-start.11 = (f32[4096]{0:T(1024)S(1)}, f32[4096]{0:T(1024)S(1)}, u32[]{:S(2)}, u32[]{:S(2)}) collective-permute-start(f32[4096]{0:T(1024)S(1)} %multiply_multiply_fusion), channel_id=1, source_target_pairs={{1,0},{2,1},{3,2},{4,3},{5,4},{6,5},{7,6},{8,7},{9,8},{10,9},{11,1... | collective-permute-start | bytes 49160 | tf_op jit(solution)/shard_map/ppermute | solution.py:169
  132.8 3.1 %collective-permute-start.9 = (s32[4096]{0:T(1024)S(1)}, s32[4096]{0:T(1024)S(1)}, u32[]{:S(2)}, u32[]{:S(2)}) collective-permute-start(s32[4096]{0:T(1024)S(1)} %copy-done.3), channel_id=1, source_target_pairs={{1,0},{2,1},{3,2},{4,3},{5,4},{6,5},{7,6},{8,7},{9,8},{10,9},{11,1... | collective-permute-start | bytes 49160 | tf_op jit(solution)/shard_map/ppermute | solution.py:169
  135.9 0.0 collective-permute-done.8
  135.9 2.5 %collective-permute-done.9 = s32[4096]{0:T(1024)S(1)} collective-permute-done((s32[4096]{0:T(1024)S(1)}, s32[4096]{0:T(1024)S(1)}, u32[]{:S(2)}, u32[]{:S(2)}) %collective-permute-start.9) | collective-permute-done | bytes 16416 | tf_op jit(solution)/shard_map/ppermute | solution.py:169
  138.4 0.0 collective-permute-done.10
  138.5 0.0 collective-permute-done.11
  138.5 29.0 %shard_map.128 = bf16[11776,128]{1,0:T(8,128)(2,1)S(1)} custom-call(s32[12288]{0:T(1024)S(1)} %get-tuple-element.21.index_ref, s32[12288]{0:T(1024)S(1)} %get-tuple-element.20.lane_ref, f32[12288]{0:T(1024)S(1)} %pad_maximum_fusion.value_ref), custom_call_target="tpu_custom_call" | custom-call | tf_op jit(solution)/shard_map/pallas_call | solution.py:148
  167.5 3.2 %reshape.72 = bf16[46,32768]{1,0:T(8,128)(2,1)} reshape(bf16[11776,128]{1,0:T(8,128)(2,1)S(1)} %shard_map.128) | data formatting | bytes 6029312 | tf_op jit(solution)/shard_map/reshape.7
  170.7 2.4 %fusion = bf16[1,16,32768]{2,1,0:T(8,128)(2,1)S(1)} fusion(bf16[46,32768]{1,0:T(8,128)(2,1)} %reshape.72, bf16[16,46]{1,0:T(8,128)(2,1)S(1)} %copy-done.7), kind=kOutput, calls=%fused_computation.3 | convolution fusion | flops 48758784 | bytes 4064704 | tf_op jit(solution)/shard_map/ip,mpc->mic/dot_general | solution.py:66
  173.1 2.3 %reshape.73 = bf16[16,512,64]{2,1,0:T(8,128)(2,1)S(1)} reshape(bf16[1,16,32768]{2,1,0:T(8,128)(2,1)S(1)} %fusion) | data formatting | bytes 2097152 | tf_op jit(solution)/shard_map/reshape.9
  175.4 4.9 %fusion.8 = f32[16,512,64]{2,1,0:T(8,128)} fusion(bf16[64,64,1]{1,0,2:T(8,128)(2,1)S(1)} %copy-done.2, bf16[16,512,64]{2,1,0:T(8,128)(2,1)S(1)} %reshape.73, bf16[512,512,1]{1,0,2:T(8,128)(2,1)} %constant.100), kind=kOutput, calls=%fused_computation.19 | convolution fusion | flops 604504064 | bytes 3678208 | tf_op jit(solution)/shard_map/mxyq,zq->mxyz/dot_general | solution.py:52
  180.3 3.0 %reshape.75 = f32[1,16,32768]{2,1,0:T(8,128)S(1)} reshape(f32[16,512,64]{2,1,0:T(8,128)} %fusion.8) | data formatting | bytes 4194304 | tf_op jit(solution)/shard_map/reshape | solution.py:53
  183.3 1.5 convert_add_fusion
  (19 shorter events, 0.2 us)
Async XLA Ops:
  0.0 3.1 %copy-start.2 = (bf16[64,64,1]{1,0,2:T(8,128)(2,1)S(1)}, bf16[64,64,1]{1,0,2:T(8,128)(2,1)}, u32[]{:S(2)}) copy-start(bf16[64,64,1]{1,0,2:T(8,128)(2,1)} %constant.99) | copy-start | bytes 24580
  9.9 37.5 %collective-permute-start = (bf16[1,15,32768]{2,1,0:T(8,128)(2,1)}, bf16[1,15,32768]{2,1,0:T(8,128)(2,1)}, u32[]{:S(2)}, u32[]{:S(2)}) collective-permute-start(bf16[1,15,32768]{2,1,0:T(8,128)(2,1)} %get-tuple-element.11), channel_id=1, source_target_pairs={{0,1},{1,2},{2,3},{3,4},{4,5},{5,6},{6,7},{7,8},{8,9},{9,10},{10,1... | collective-permute-start | bytes 2949128 | tf_op jit(solution)/shard_map/ppermute | solution.py:23
  13.7 14.2 %copy-start.3 = (s32[4096]{0:T(1024)S(1)}, s32[4096]{0:T(1024)}, u32[]{:S(2)}) copy-start(s32[4096]{0:T(1024)} %param.15) | copy-start | bytes 49156
  13.7 14.2 %copy-start.4 = (s32[4096]{0:T(1024)S(1)}, s32[4096]{0:T(1024)}, u32[]{:S(2)}) copy-start(s32[4096]{0:T(1024)} %param.16) | copy-start | bytes 49156
  13.7 49.5 %collective-permute-start.1 = (bf16[1,15,32768]{2,1,0:T(8,128)(2,1)}, bf16[1,15,32768]{2,1,0:T(8,128)(2,1)}, u32[]{:S(2)}, u32[]{:S(2)}) collective-permute-start(bf16[1,15,32768]{2,1,0:T(8,128)(2,1)} %get-tuple-element.12), channel_id=1, source_target_pairs={{1,0},{2,1},{3,2},{4,3},{5,4},{6,5},{7,6},{8,7},{9,8},{10,9},{11,1... | collective-permute-start | bytes 2949128 | tf_op jit(solution)/shard_map/ppermute | solution.py:26
  27.9 35.3 %copy-start.7 = (bf16[16,46]{1,0:T(8,128)(2,1)S(1)}, bf16[16,46]{1,0:T(8,128)(2,1)}, u32[]{:S(2)}) copy-start(bf16[16,46]{1,0:T(8,128)(2,1)} %constant.95.clone) | copy-start | bytes 4420
  68.8 6.0 %copy-start.1 = (bf16[4096,128]{1,0:T(8,128)(2,1)S(1)}, bf16[4096,128]{1,0:T(8,128)(2,1)}, u32[]{:S(2)}) copy-start(bf16[4096,128]{1,0:T(8,128)(2,1)} %gather_fusion) | copy-start | bytes 3145732
  74.7 41.7 %copy-start.5 = (f32[4096]{0:T(1024)S(1)}, f32[4096]{0:T(1024)}, u32[]{:S(2)}) copy-start(f32[4096]{0:T(1024)} %param.17) | copy-start | bytes 49156
  74.7 41.7 %copy-start.6 = (f32[4096]{0:T(1024)S(1)}, f32[4096]{0:T(1024)}, u32[]{:S(2)}) copy-start(f32[4096]{0:T(1024)} %param.18) | copy-start | bytes 49156
  76.4 7.6 %collective-permute-start.2 = (f32[4096]{0:T(1024)S(1)}, f32[4096]{0:T(1024)S(1)}, u32[]{:S(2)}, u32[]{:S(2)}) collective-permute-start(f32[4096]{0:T(1024)S(1)} %mul.21), channel_id=1, source_target_pairs={{0,96},{32,64},{64,32},{96,0},{128,224},{160,192},{192,160},{224,1... | collective-permute-start | bytes 49160 | tf_op jit(solution)/shard_map/ppermute | solution.py:76
  78.3 5.7 %collective-permute-start.3 = (f32[4096]{0:T(1024)S(1)}, f32[4096]{0:T(1024)S(1)}, u32[]{:S(2)}, u32[]{:S(2)}) collective-permute-start(f32[4096]{0:T(1024)S(1)} %mul.21), channel_id=1, source_target_pairs={{0,64},{32,96},{64,0},{96,32},{128,192},{160,224},{192,128},{224,1... | collective-permute-start | bytes 49160 | tf_op jit(solution)/shard_map/ppermute | solution.py:76
  81.8 3.1 %collective-permute-start.4 = (f32[4096]{0:T(1024)S(1)}, f32[4096]{0:T(1024)S(1)}, u32[]{:S(2)}, u32[]{:S(2)}) collective-permute-start(f32[4096]{0:T(1024)S(1)} %mul.21), channel_id=1, source_target_pairs={{0,32},{32,0},{64,96},{96,64},{128,160},{160,128},{192,224},{224,1... | collective-permute-start | bytes 49160 | tf_op jit(solution)/shard_map/ppermute | solution.py:76
  84.9 22.3 %collective-permute-start.5 = (f32[4096]{0:T(1024)S(1)}, f32[4096]{0:T(1024)S(1)}, u32[]{:S(2)}, u32[]{:S(2)}) collective-permute-start(f32[4096]{0:T(1024)S(1)} %select_add_fusion), channel_id=1, source_target_pairs={{0,384},{32,416},{64,448},{96,480},{128,256},{160,288},{192,320},{... | collective-permute-start | bytes 49160 | tf_op jit(solution)/shard_map/ppermute | solution.py:76
  102.1 14.3 %collective-permute-start.6 = (f32[4096]{0:T(1024)S(1)}, f32[4096]{0:T(1024)S(1)}, u32[]{:S(2)}, u32[]{:S(2)}) collective-permute-start(f32[4096]{0:T(1024)S(1)} %select_add_fusion), channel_id=1, source_target_pairs={{0,256},{32,288},{64,320},{96,352},{128,384},{160,416},{192,448},{... | collective-permute-start | bytes 49160 | tf_op jit(solution)/shard_map/ppermute | solution.py:76
  104.0 12.4 %collective-permute-start.7 = (f32[4096]{0:T(1024)S(1)}, f32[4096]{0:T(1024)S(1)}, u32[]{:S(2)}, u32[]{:S(2)}) collective-permute-start(f32[4096]{0:T(1024)S(1)} %select_add_fusion), channel_id=1, source_target_pairs={{0,128},{32,160},{64,192},{96,224},{128,0},{160,32},{192,64},{224,... | collective-permute-start | bytes 49160 | tf_op jit(solution)/shard_map/ppermute | solution.py:76
  116.5 19.4 %collective-permute-start.8 = (s32[4096]{0:T(1024)S(1)}, s32[4096]{0:T(1024)S(1)}, u32[]{:S(2)}, u32[]{:S(2)}) collective-permute-start(s32[4096]{0:T(1024)S(1)} %copy-done.3), channel_id=1, source_target_pairs={{0,1},{1,2},{2,3},{3,4},{4,5},{5,6},{6,7},{7,8},{8,9},{9,10},{10,1... | collective-permute-start | bytes 49160 | tf_op jit(solution)/shard_map/ppermute | solution.py:168
  119.4 19.1 %collective-permute-start.10 = (f32[4096]{0:T(1024)S(1)}, f32[4096]{0:T(1024)S(1)}, u32[]{:S(2)}, u32[]{:S(2)}) collective-permute-start(f32[4096]{0:T(1024)S(1)} %multiply_multiply_fusion), channel_id=1, source_target_pairs={{0,1},{1,2},{2,3},{3,4},{4,5},{5,6},{6,7},{7,8},{8,9},{9,10},{10,1... | collective-permute-start | bytes 49160 | tf_op jit(solution)/shard_map/ppermute | solution.py:168
  122.5 16.0 %collective-permute-start.11 = (f32[4096]{0:T(1024)S(1)}, f32[4096]{0:T(1024)S(1)}, u32[]{:S(2)}, u32[]{:S(2)}) collective-permute-start(f32[4096]{0:T(1024)S(1)} %multiply_multiply_fusion), channel_id=1, source_target_pairs={{1,0},{2,1},{3,2},{4,3},{5,4},{6,5},{7,6},{8,7},{9,8},{10,9},{11,1... | collective-permute-start | bytes 49160 | tf_op jit(solution)/shard_map/ppermute | solution.py:169
  132.8 5.6 %collective-permute-start.9 = (s32[4096]{0:T(1024)S(1)}, s32[4096]{0:T(1024)S(1)}, u32[]{:S(2)}, u32[]{:S(2)}) collective-permute-start(s32[4096]{0:T(1024)S(1)} %copy-done.3), channel_id=1, source_target_pairs={{1,0},{2,1},{3,2},{4,3},{5,4},{6,5},{7,6},{8,7},{9,8},{10,9},{11,1... | collective-permute-start | bytes 49160 | tf_op jit(solution)/shard_map/ppermute | solution.py:169
  180.3 3.0 %copy-start = (bf16[1,16,32768]{2,1,0:T(8,128)(2,1)S(1)}, bf16[1,16,32768]{2,1,0:T(8,128)(2,1)}, u32[]{:S(2)}) copy-start(bf16[1,16,32768]{2,1,0:T(8,128)(2,1)} %param.13) | copy-start | bytes 3145732

commit v6 on v4

--- a/solution.py
+++ b/solution.py
@@ -196,7 +196,7 @@
     ])
     all_contrib = jnp.concatenate([left_contrib, contrib, right_contrib])
     extended = scatter_regions(
-        all_row, all_cell % LANES, all_contrib, (halo_rows, rows, halo_rows), 2
+        all_row, all_cell % LANES, all_contrib, (halo_rows, rows, halo_rows), 4
     )
     padded_back = extended.reshape(members, slab_rows + 2 * tap_reach, plane_cells)
     x_back = along_x(padded_back, slab_rows).astype(jnp.bfloat16)

time: 179 us -> 178 us (level)
  no operation moved by 1% of the time
where the time goes in v6:
time: 178 us; the launch traced here: 177 us
  waiting for transfers between devices  54.8 us (31%)
  starting transfers between devices  35.6 us (20%)
  local copies, waits for them, and re-layouts  35.5 us (20%)
  Pallas kernels  33.6 us (19%)
  matrix products  13.6 us (8%)
  other arithmetic  3.2 us (2%)
    pallas_call x1, Pallas kernels, scatter_regions(): pl.pallas_call(kernel, out_shape=jax.ShapeDtypeStruct((total_rows, LANES)...  27.6 us
    ppermute x1, waiting for transfers between devices, padded_2(): lax.ppermute(lax.slice_in_dim(block, 0, width, axis=dim), axis, backward)  22.8 us
    ppermute x4, waiting for transfers between devices, butterfly_sum(): partner = lax.ppermute(value, axis, [(i, i ^ step) for i in range(count)])  17.1 us
    gather x1, local copies, waits for them, and re-layouts, local(): perturbations.reshape(slot_count * rows, LANES)[obs_slot * rows + obs_row]  15 us
    ppermute x4, starting transfers between devices, butterfly_sum(): partner = lax.ppermute(value, axis, [(i, i ^ step) for i in range(count)])  12.4 us
    ppermute x2, waiting for transfers between devices, neighbours(): lax.ppermute(value, axis, [(i + 1, i) for i in range(count - 1)])  11 us
    ppermute x2, starting transfers between devices, neighbours(): lax.ppermute(value, axis, [(i, i + 1) for i in range(count - 1)])  8.52 us
    ppermute x1, starting transfers between devices, padded_2(): lax.ppermute(lax.slice_in_dim(block, block.shape[dim] - width, None, axis...  7.71 us
  transfers between devices with their start and end apart: 10, of which 7 were waited for; matrix products, arithmetic and copies ran while one was open for 10% of the time, Pallas kernels for 0%

profile of v6, /device:TPU:480, one launch (start us, length us, event | category | flops | bytes accessed | tf_op | source)
XLA Modules:
  0.0 177.2 jit_solution(1922592258102900945)
XLA Ops:
  0.0 3.0 %reshape.69 = bf16[16,512,64]{2,1,0:T(8,128)(2,1)S(1)} reshape(bf16[1,16,32768]{2,1,0:T(8,128)(2,1)} %param.13) | data formatting | bytes 2097152 | tf_op jit(solution)/shard_map/reshape
  3.1 0.0 copy-done.2
  3.1 2.5 %fusion.7 = bf16[1,16,512,64]{2,3,1,0:T(8,128)(2,1)S(1)} fusion(bf16[512,512,1]{1,0,2:T(8,128)(2,1)} %constant.83, bf16[64,64,1]{1,0,2:T(8,128)(2,1)S(1)} %copy-done.2, bf16[16,512,64]{2,1,0:T(8,128)(2,1)S(1)} %reshape.69), kind=kOutput, calls=%fused_computation.18 | convolution fusion | flops 605028352 | bytes 2629632 | tf_op jit(solution)/shard_map/mxqz,yq->mxyz/dot_general | solution.py:60
  5.6 1.1 copy.15
  6.6 1.7 convert_element_type.68
  8.3 1.5 fusion.24
  9.9 7.7 %collective-permute-start = (bf16[1,15,32768]{2,1,0:T(8,128)(2,1)}, bf16[1,15,32768]{2,1,0:T(8,128)(2,1)}, u32[]{:S(2)}, u32[]{:S(2)}) collective-permute-start(bf16[1,15,32768]{2,1,0:T(8,128)(2,1)} %get-tuple-element.11), channel_id=1, source_target_pairs={{0,1},{1,2},{2,3},{3,4},{4,5},{5,6},{6,7},{7,8},{8,9},{9,10},{10,1... | collective-permute-start | bytes 2949128 | tf_op jit(solution)/shard_map/ppermute | solution.py:23
  17.6 0.0 copy-start.3
  17.6 0.0 copy-start.4
  17.6 1.9 %collective-permute-start.1 = (bf16[1,15,32768]{2,1,0:T(8,128)(2,1)}, bf16[1,15,32768]{2,1,0:T(8,128)(2,1)}, u32[]{:S(2)}, u32[]{:S(2)}) collective-permute-start(bf16[1,15,32768]{2,1,0:T(8,128)(2,1)} %get-tuple-element.12), channel_id=1, source_target_pairs={{1,0},{2,1},{3,2},{4,3},{5,4},{6,5},{7,6},{8,7},{9,8},{10,9},{11,1... | collective-permute-start | bytes 2949128 | tf_op jit(solution)/shard_map/ppermute | solution.py:26
  19.6 2.9 %reshape.68 = bf16[8192,128]{1,0:T(8,128)(2,1)S(1)} reshape(bf16[2,1,16,32768]{3,2,1,0:T(8,128)(2,1)} %param.14) | data formatting | bytes 4194304 | tf_op jit(solution)/shard_map/reshape | solution.py:174
  22.4 0.0 copy-done.3
  22.5 0.0 copy-done.4
  22.5 0.0 copy-start.7
  22.5 15.0 %gather_fusion = bf16[4096,128]{1,0:T(8,128)(2,1)} fusion(bf16[8192,128]{1,0:T(8,128)(2,1)S(1)} %reshape.68, s32[4096]{0:T(1024)S(1)} %get-tuple-element.17), kind=kCustom, calls=%fused_computation | custom fusion | bytes 2113536 | tf_op jit(solution)/shard_map/gather | solution.py:174
  37.5 3.9 %collective-permute-done = bf16[1,15,32768]{2,1,0:T(8,128)(2,1)} collective-permute-done((bf16[1,15,32768]{2,1,0:T(8,128)(2,1)}, bf16[1,15,32768]{2,1,0:T(8,128)(2,1)}, u32[]{:S(2)}, u32[]{:S(2)}) %collective-permute-start) | collective-permute-done | bytes 983072 | tf_op jit(solution)/shard_map/ppermute | solution.py:23
  41.4 22.8 %collective-permute-done.1 = bf16[1,15,32768]{2,1,0:T(8,128)(2,1)} collective-permute-done((bf16[1,15,32768]{2,1,0:T(8,128)(2,1)}, bf16[1,15,32768]{2,1,0:T(8,128)(2,1)}, u32[]{:S(2)}, u32[]{:S(2)}) %collective-permute-start.1) | collective-permute-done | bytes 983072 | tf_op jit(solution)/shard_map/ppermute | solution.py:26
  64.3 3.8 %convolution_bitcast_fusion = f32[1,16,32768]{2,1,0:T(8,128)} fusion(bf16[16,46]{1,0:T(8,128)(2,1)S(1)} %copy-done.7, bf16[1,15,32768]{2,1,0:T(8,128)(2,1)} %collective-permute-done.1, bf16[1,16,32768]{2,1,0:T(8,128)(2,1)S(1)} %convert_element_type.68, bf16[1,15,32768]{2,1,0:T(8,128)(2,1)} %collective-permute-done), kind=kOutput, calls=%fused_computation.1 | convolution fusion | flops 57278464 | bytes 5113280 | tf_op jit(solution)/shard_map/ip,mpc->mic/dot_general | solution.py:66
  68.1 1.7 reshape.71.field_ref
  69.8 5.9 %shard_map.127 = f32[4096,128]{1,0:T(8,128)S(1)} custom-call(s32[4096]{0:T(1024)S(1)} %get-tuple-element.18.index_ref, f32[4096,128]{1,0:T(8,128)S(1)} %reshape.71.field_ref), custom_call_target="tpu_custom_call" | custom-call | tf_op jit(solution)/shard_map/pallas_call | solution.py:91
  75.8 0.0 copy-start.5
  75.8 0.0 copy-start.6
  75.8 0.0 copy-done.1
  75.8 1.6 select_reduce_fusion
  77.4 1.9 %collective-permute-start.2 = (f32[4096]{0:T(1024)S(1)}, f32[4096]{0:T(1024)S(1)}, u32[]{:S(2)}, u32[]{:S(2)}) collective-permute-start(f32[4096]{0:T(1024)S(1)} %mul.21), channel_id=1, source_target_pairs={{0,32},{32,0},{64,96},{96,64},{128,160},{160,128},{192,224},{224,1... | collective-permute-start | bytes 49160 | tf_op jit(solution)/shard_map/ppermute | solution.py:73
  79.3 1.1 collective-permute-done.2
  80.5 3.5 %collective-permute-start.3 = (f32[4096]{0:T(1024)S(1)}, f32[4096]{0:T(1024)S(1)}, u32[]{:S(2)}, u32[]{:S(2)}) collective-permute-start(f32[4096]{0:T(1024)S(1)} %add.44), channel_id=1, source_target_pairs={{0,64},{32,96},{64,0},{96,32},{128,192},{160,224},{192,128},{224,1... | collective-permute-start | bytes 49160 | tf_op jit(solution)/shard_map/ppermute | solution.py:73
  83.9 2.1 %collective-permute-done.3 = f32[4096]{0:T(1024)S(1)} collective-permute-done((f32[4096]{0:T(1024)S(1)}, f32[4096]{0:T(1024)S(1)}, u32[]{:S(2)}, u32[]{:S(2)}) %collective-permute-start.3) | collective-permute-done | bytes 16416 | tf_op jit(solution)/shard_map/ppermute | solution.py:73
  86.1 5.1 %collective-permute-start.4 = (f32[4096]{0:T(1024)S(1)}, f32[4096]{0:T(1024)S(1)}, u32[]{:S(2)}, u32[]{:S(2)}) collective-permute-start(f32[4096]{0:T(1024)S(1)} %add.45), channel_id=1, source_target_pairs={{0,128},{32,160},{64,192},{96,224},{128,0},{160,32},{192,64},{224,... | collective-permute-start | bytes 49160 | tf_op jit(solution)/shard_map/ppermute | solution.py:73
  91.2 2.0 %collective-permute-done.4 = f32[4096]{0:T(1024)S(1)} collective-permute-done((f32[4096]{0:T(1024)S(1)}, f32[4096]{0:T(1024)S(1)}, u32[]{:S(2)}, u32[]{:S(2)}) %collective-permute-start.4) | collective-permute-done | bytes 16416 | tf_op jit(solution)/shard_map/ppermute | solution.py:73
  93.2 1.9 %collective-permute-start.5 = (f32[4096]{0:T(1024)S(1)}, f32[4096]{0:T(1024)S(1)}, u32[]{:S(2)}, u32[]{:S(2)}) collective-permute-start(f32[4096]{0:T(1024)S(1)} %add.46), channel_id=1, source_target_pairs={{0,256},{32,288},{64,320},{96,352},{128,384},{160,416},{192,448},{... | collective-permute-start | bytes 49160 | tf_op jit(solution)/shard_map/ppermute | solution.py:73
  95.8 11.8 %collective-permute-done.5 = f32[4096]{0:T(1024)S(1)} collective-permute-done((f32[4096]{0:T(1024)S(1)}, f32[4096]{0:T(1024)S(1)}, u32[]{:S(2)}, u32[]{:S(2)}) %collective-permute-start.5) | collective-permute-done | bytes 16416 | tf_op jit(solution)/shard_map/ppermute | solution.py:73
  107.6 0.0 copy-done.6
  107.6 5.6 %collective-permute-start.6 = (s32[4096]{0:T(1024)S(1)}, s32[4096]{0:T(1024)S(1)}, u32[]{:S(2)}, u32[]{:S(2)}) collective-permute-start(s32[4096]{0:T(1024)S(1)} %copy-done.3), channel_id=1, source_target_pairs={{0,1},{1,2},{2,3},{3,4},{4,5},{5,6},{6,7},{7,8},{8,9},{9,10},{10,1... | collective-permute-start | bytes 49160 | tf_op jit(solution)/shard_map/ppermute | solution.py:155
  113.2 2.9 %collective-permute-start.8 = (f32[4096]{0:T(1024)S(1)}, f32[4096]{0:T(1024)S(1)}, u32[]{:S(2)}, u32[]{:S(2)}) collective-permute-start(f32[4096]{0:T(1024)S(1)} %multiply_multiply_fusion), channel_id=1, source_target_pairs={{0,1},{1,2},{2,3},{3,4},{4,5},{5,6},{6,7},{7,8},{8,9},{9,10},{10,1... | collective-permute-start | bytes 49160 | tf_op jit(solution)/shard_map/ppermute | solution.py:155
  116.1 2.9 %collective-permute-start.9 = (f32[4096]{0:T(1024)S(1)}, f32[4096]{0:T(1024)S(1)}, u32[]{:S(2)}, u32[]{:S(2)}) collective-permute-start(f32[4096]{0:T(1024)S(1)} %multiply_multiply_fusion), channel_id=1, source_target_pairs={{1,0},{2,1},{3,2},{4,3},{5,4},{6,5},{7,6},{8,7},{9,8},{10,9},{11,1... | collective-permute-start | bytes 49160 | tf_op jit(solution)/shard_map/ppermute | solution.py:156
  119.0 2.1 %collective-permute-start.7 = (s32[4096]{0:T(1024)S(1)}, s32[4096]{0:T(1024)S(1)}, u32[]{:S(2)}, u32[]{:S(2)}) collective-permute-start(s32[4096]{0:T(1024)S(1)} %copy-done.3), channel_id=1, source_target_pairs={{1,0},{2,1},{3,2},{4,3},{5,4},{6,5},{7,6},{8,7},{9,8},{10,9},{11,1... | collective-permute-start | bytes 49160 | tf_op jit(solution)/shard_map/ppermute | solution.py:156
  121.2 0.0 collective-permute-done.6
  121.2 11.0 %collective-permute-done.7 = s32[4096]{0:T(1024)S(1)} collective-permute-done((s32[4096]{0:T(1024)S(1)}, s32[4096]{0:T(1024)S(1)}, u32[]{:S(2)}, u32[]{:S(2)}) %collective-permute-start.7) | collective-permute-done | bytes 16416 | tf_op jit(solution)/shard_map/ppermute | solution.py:156
  132.2 0.0 collective-permute-done.8
  132.2 0.0 collective-permute-done.9
  132.3 27.6 %shard_map.128 = bf16[11776,128]{1,0:T(8,128)(2,1)S(1)} custom-call(s32[12288]{0:T(1024)S(1)} %get-tuple-element.21.index_ref, s32[12288]{0:T(1024)S(1)} %get-tuple-element.20.lane_ref, f32[12288]{0:T(1024)S(1)} %pad_maximum_fusion.value_ref), custom_call_target="tpu_custom_call" | custom-call | tf_op jit(solution)/shard_map/pallas_call | solution.py:135
  159.9 3.2 %reshape.72 = bf16[46,32768]{1,0:T(8,128)(2,1)} reshape(bf16[11776,128]{1,0:T(8,128)(2,1)S(1)} %shard_map.128) | data formatting | bytes 6029312 | tf_op jit(solution)/shard_map/reshape.7
  163.1 2.4 %fusion = bf16[1,16,32768]{2,1,0:T(8,128)(2,1)S(1)} fusion(bf16[46,32768]{1,0:T(8,128)(2,1)} %reshape.72, bf16[16,46]{1,0:T(8,128)(2,1)S(1)} %copy-done.7), kind=kOutput, calls=%fused_computation.3 | convolution fusion | flops 48758784 | bytes 4064704 | tf_op jit(solution)/shard_map/ip,mpc->mic/dot_general | solution.py:66
  165.5 2.3 %reshape.73 = bf16[16,512,64]{2,1,0:T(8,128)(2,1)S(1)} reshape(bf16[1,16,32768]{2,1,0:T(8,128)(2,1)S(1)} %fusion) | data formatting | bytes 2097152 | tf_op jit(solution)/shard_map/reshape.9
  167.8 4.9 %fusion.8 = f32[16,512,64]{2,1,0:T(8,128)} fusion(bf16[64,64,1]{1,0,2:T(8,128)(2,1)S(1)} %copy-done.2, bf16[16,512,64]{2,1,0:T(8,128)(2,1)S(1)} %reshape.73, bf16[512,512,1]{1,0,2:T(8,128)(2,1)} %constant.83), kind=kOutput, calls=%fused_computation.19 | convolution fusion | flops 604504064 | bytes 3678208 | tf_op jit(solution)/shard_map/mxyq,zq->mxyz/dot_general | solution.py:52
  172.7 3.0 %reshape.75 = f32[1,16,32768]{2,1,0:T(8,128)S(1)} reshape(f32[16,512,64]{2,1,0:T(8,128)} %fusion.8) | data formatting | bytes 4194304 | tf_op jit(solution)/shard_map/reshape | solution.py:53
  175.7 1.5 convert_add_fusion
  (17 shorter events, 0.1 us)
Async XLA Ops:
  0.0 3.1 %copy-start.2 = (bf16[64,64,1]{1,0,2:T(8,128)(2,1)S(1)}, bf16[64,64,1]{1,0,2:T(8,128)(2,1)}, u32[]{:S(2)}) copy-start(bf16[64,64,1]{1,0,2:T(8,128)(2,1)} %constant.82) | copy-start | bytes 24580
  9.9 31.6 %collective-permute-start = (bf16[1,15,32768]{2,1,0:T(8,128)(2,1)}, bf16[1,15,32768]{2,1,0:T(8,128)(2,1)}, u32[]{:S(2)}, u32[]{:S(2)}) collective-permute-start(bf16[1,15,32768]{2,1,0:T(8,128)(2,1)} %get-tuple-element.11), channel_id=1, source_target_pairs={{0,1},{1,2},{2,3},{3,4},{4,5},{5,6},{6,7},{7,8},{8,9},{9,10},{10,1... | collective-permute-start | bytes 2949128 | tf_op jit(solution)/shard_map/ppermute | solution.py:23
  17.6 4.8 %copy-start.3 = (s32[4096]{0:T(1024)S(1)}, s32[4096]{0:T(1024)}, u32[]{:S(2)}) copy-start(s32[4096]{0:T(1024)} %param.15) | copy-start | bytes 49156
  17.6 4.8 %copy-start.4 = (s32[4096]{0:T(1024)S(1)}, s32[4096]{0:T(1024)}, u32[]{:S(2)}) copy-start(s32[4096]{0:T(1024)} %param.16) | copy-start | bytes 49156
  17.6 46.6 %collective-permute-start.1 = (bf16[1,15,32768]{2,1,0:T(8,128)(2,1)}, bf16[1,15,32768]{2,1,0:T(8,128)(2,1)}, u32[]{:S(2)}, u32[]{:S(2)}) collective-permute-start(bf16[1,15,32768]{2,1,0:T(8,128)(2,1)} %get-tuple-element.12), channel_id=1, source_target_pairs={{1,0},{2,1},{3,2},{4,3},{5,4},{6,5},{7,6},{8,7},{9,8},{10,9},{11,1... | collective-permute-start | bytes 2949128 | tf_op jit(solution)/shard_map/ppermute | solution.py:26
  22.5 41.8 %copy-start.7 = (bf16[16,46]{1,0:T(8,128)(2,1)S(1)}, bf16[16,46]{1,0:T(8,128)(2,1)}, u32[]{:S(2)}) copy-start(bf16[16,46]{1,0:T(8,128)(2,1)} %constant.78.clone) | copy-start | bytes 4420
  69.8 6.0 %copy-start.1 = (bf16[4096,128]{1,0:T(8,128)(2,1)S(1)}, bf16[4096,128]{1,0:T(8,128)(2,1)}, u32[]{:S(2)}) copy-start(bf16[4096,128]{1,0:T(8,128)(2,1)} %gather_fusion) | copy-start | bytes 3145732
  75.8 31.8 %copy-start.5 = (f32[4096]{0:T(1024)S(1)}, f32[4096]{0:T(1024)}, u32[]{:S(2)}) copy-start(f32[4096]{0:T(1024)} %param.17) | copy-start | bytes 49156
  75.8 31.8 %copy-start.6 = (f32[4096]{0:T(1024)S(1)}, f32[4096]{0:T(1024)}, u32[]{:S(2)}) copy-start(f32[4096]{0:T(1024)} %param.18) | copy-start | bytes 49156
  77.4 3.1 %collective-permute-start.2 = (f32[4096]{0:T(1024)S(1)}, f32[4096]{0:T(1024)S(1)}, u32[]{:S(2)}, u32[]{:S(2)}) collective-permute-start(f32[4096]{0:T(1024)S(1)} %mul.21), channel_id=1, source_target_pairs={{0,32},{32,0},{64,96},{96,64},{128,160},{160,128},{192,224},{224,1... | collective-permute-start | bytes 49160 | tf_op jit(solution)/shard_map/ppermute | solution.py:73
  80.5 5.6 %collective-permute-start.3 = (f32[4096]{0:T(1024)S(1)}, f32[4096]{0:T(1024)S(1)}, u32[]{:S(2)}, u32[]{:S(2)}) collective-permute-start(f32[4096]{0:T(1024)S(1)} %add.44), channel_id=1, source_target_pairs={{0,64},{32,96},{64,0},{96,32},{128,192},{160,224},{192,128},{224,1... | collective-permute-start | bytes 49160 | tf_op jit(solution)/shard_map/ppermute | solution.py:73
  86.1 7.1 %collective-permute-start.4 = (f32[4096]{0:T(1024)S(1)}, f32[4096]{0:T(1024)S(1)}, u32[]{:S(2)}, u32[]{:S(2)}) collective-permute-start(f32[4096]{0:T(1024)S(1)} %add.45), channel_id=1, source_target_pairs={{0,128},{32,160},{64,192},{96,224},{128,0},{160,32},{192,64},{224,... | collective-permute-start | bytes 49160 | tf_op jit(solution)/shard_map/ppermute | solution.py:73
  93.2 14.3 %collective-permute-start.5 = (f32[4096]{0:T(1024)S(1)}, f32[4096]{0:T(1024)S(1)}, u32[]{:S(2)}, u32[]{:S(2)}) collective-permute-start(f32[4096]{0:T(1024)S(1)} %add.46), channel_id=1, source_target_pairs={{0,256},{32,288},{64,320},{96,352},{128,384},{160,416},{192,448},{... | collective-permute-start | bytes 49160 | tf_op jit(solution)/shard_map/ppermute | solution.py:73
  107.6 13.6 %collective-permute-start.6 = (s32[4096]{0:T(1024)S(1)}, s32[4096]{0:T(1024)S(1)}, u32[]{:S(2)}, u32[]{:S(2)}) collective-permute-start(s32[4096]{0:T(1024)S(1)} %copy-done.3), channel_id=1, source_target_pairs={{0,1},{1,2},{2,3},{3,4},{4,5},{5,6},{6,7},{7,8},{8,9},{9,10},{10,1... | collective-permute-start | bytes 49160 | tf_op jit(solution)/shard_map/ppermute | solution.py:155
  113.2 19.1 %collective-permute-start.8 = (f32[4096]{0:T(1024)S(1)}, f32[4096]{0:T(1024)S(1)}, u32[]{:S(2)}, u32[]{:S(2)}) collective-permute-start(f32[4096]{0:T(1024)S(1)} %multiply_multiply_fusion), channel_id=1, source_target_pairs={{0,1},{1,2},{2,3},{3,4},{4,5},{5,6},{6,7},{7,8},{8,9},{9,10},{10,1... | collective-permute-start | bytes 49160 | tf_op jit(solution)/shard_map/ppermute | solution.py:155
  116.1 16.1 %collective-permute-start.9 = (f32[4096]{0:T(1024)S(1)}, f32[4096]{0:T(1024)S(1)}, u32[]{:S(2)}, u32[]{:S(2)}) collective-permute-start(f32[4096]{0:T(1024)S(1)} %multiply_multiply_fusion), channel_id=1, source_target_pairs={{1,0},{2,1},{3,2},{4,3},{5,4},{6,5},{7,6},{8,7},{9,8},{10,9},{11,1... | collective-permute-start | bytes 49160 | tf_op jit(solution)/shard_map/ppermute | solution.py:156
  119.0 13.1 %collective-permute-start.7 = (s32[4096]{0:T(1024)S(1)}, s32[4096]{0:T(1024)S(1)}, u32[]{:S(2)}, u32[]{:S(2)}) collective-permute-start(s32[4096]{0:T(1024)S(1)} %copy-done.3), channel_id=1, source_target_pairs={{1,0},{2,1},{3,2},{4,3},{5,4},{6,5},{7,6},{8,7},{9,8},{10,9},{11,1... | collective-permute-start | bytes 49160 | tf_op jit(solution)/shard_map/ppermute | solution.py:156
  172.7 3.0 %copy-start = (bf16[1,16,32768]{2,1,0:T(8,128)(2,1)S(1)}, bf16[1,16,32768]{2,1,0:T(8,128)(2,1)}, u32[]{:S(2)}) copy-start(bf16[1,16,32768]{2,1,0:T(8,128)(2,1)} %param.13) | copy-start | bytes 3145732

commit v7 on v6

--- a/solution.py
+++ b/solution.py
@@ -101,13 +101,13 @@
     )(index, field)
 
 
-def scatter_regions(index, lane, value, region_rows, splits):
+def scatter_regions(index, value, region_rows, splits):
     regions = len(region_rows)
     per_region = index.shape[0] // regions
     per_stream = per_region // splits
     total_rows = sum(region_rows)
 
-    def kernel(index_ref, lane_ref, value_ref, out_ref, *accs):
+    def kernel(index_ref, value_ref, out_ref, *accs):
         for acc in accs:
             acc[...] = jnp.zeros_like(acc)
         lanes = lax.broadcasted_iota(jnp.int32, (1, LANES), 1)
@@ -116,8 +116,9 @@
             for region in range(regions):
                 for split in range(splits):
                     i = region * per_region + split * per_stream + j
-                    row = index_ref[i]
-                    hit = jnp.where(lanes == lane_ref[i], value_ref[i], 0.0)
+                    code = index_ref[i]
+                    row = code // LANES
+                    hit = jnp.where(lanes == code % LANES, value_ref[i], 0.0)
                     acc = accs[region * splits + split]
                     acc[pl.ds(row, 1), :] += hit
             return carry
@@ -136,7 +137,7 @@
         kernel,
         out_shape=jax.ShapeDtypeStruct((total_rows, LANES), jnp.bfloat16),
         grid_spec=pltpu.PrefetchScalarGridSpec(
-            num_scalar_prefetch=3,
+            num_scalar_prefetch=2,
             grid=(1,),
             in_specs=[],
             out_specs=pl.BlockSpec((total_rows, LANES), lambda i, *refs: (0, 0)),
@@ -147,7 +148,7 @@
             ],
         ),
         compiler_params=pltpu.CompilerParams(vmem_limit_bytes=48 * 1024 * 1024),
-    )(index, lane, value)
+    )(index, value)
 
 
 def neighbours(value, axis):
@@ -196,7 +197,7 @@
     ])
     all_contrib = jnp.concatenate([left_contrib, contrib, right_contrib])
     extended = scatter_regions(
-        all_row, all_cell % LANES, all_contrib, (halo_rows, rows, halo_rows), 4
+        all_row * LANES + all_cell % LANES, all_contrib, (halo_rows, rows, halo_rows), 4
     )
     padded_back = extended.reshape(members, slab_rows + 2 * tap_reach, plane_cells)
     x_back = along_x(padded_back, slab_rows).astype(jnp.bfloat16)

time: 178 us -> 232 us (1.30)
  Pallas kernels: 33.6 us -> 87.5 us
    pallas_call x1, Pallas kernels: 27.6 us -> 81.5 us  [scatter_regions(): pl.pallas_call(kernel, out_shape=jax.ShapeDtypeStruct((total_rows, LANES)...]
  transfers between devices with their start and end apart: 10 -> 10, of which waited for: 7 -> 7; matrix products, arithmetic and copies ran while one was open for 10% -> 8% of each run, Pallas kernels for 0% -> 0%
where the time goes in v7:
time: 232 us; the launch traced here: 231 us
  Pallas kernels  87.5 us (38%)
  waiting for transfers between devices  54.9 us (24%)
  starting transfers between devices  35.6 us (15%)
  local copies, waits for them, and re-layouts  35.3 us (15%)
  matrix products  13.6 us (6%)
  other arithmetic  3.2 us (1%)
    pallas_call x1, Pallas kernels, scatter_regions(): pl.pallas_call(kernel, out_shape=jax.ShapeDtypeStruct((total_rows, LANES)...  81.5 us
    ppermute x1, waiting for transfers between devices, padded_2(): lax.ppermute(lax.slice_in_dim(block, 0, width, axis=dim), axis, backward)  22.8 us
    ppermute x4, waiting for transfers between devices, butterfly_sum(): partner = lax.ppermute(value, axis, [(i, i ^ step) for i in range(count)])  17.1 us
    gather x1, local copies, waits for them, and re-layouts, local(): perturbations.reshape(slot_count * rows, LANES)[obs_slot * rows + obs_row]  14.9 us
    ppermute x4, starting transfers between devices, butterfly_sum(): partner = lax.ppermute(value, axis, [(i, i ^ step) for i in range(count)])  12.4 us
    ppermute x2, waiting for transfers between devices, neighbours(): lax.ppermute(value, axis, [(i + 1, i) for i in range(count - 1)])  11 us
    ppermute x2, starting transfers between devices, neighbours(): lax.ppermute(value, axis, [(i, i + 1) for i in range(count - 1)])  8.52 us
    ppermute x1, starting transfers between devices, padded_2(): lax.ppermute(lax.slice_in_dim(block, block.shape[dim] - width, None, axis...  7.71 us
  transfers between devices with their start and end apart: 10, of which 7 were waited for; matrix products, arithmetic and copies ran while one was open for 8% of the time, Pallas kernels for 0%

profile of v7, /device:TPU:480, one launch (start us, length us, event | category | flops | bytes accessed | tf_op | source)
XLA Modules:
  0.0 231.1 jit_solution(1885710268682994308)
XLA Ops:
  0.0 3.0 %reshape.69 = bf16[16,512,64]{2,1,0:T(8,128)(2,1)S(1)} reshape(bf16[1,16,32768]{2,1,0:T(8,128)(2,1)} %param.13) | data formatting | bytes 2097152 | tf_op jit(solution)/shard_map/reshape
  3.1 0.0 copy-done.2
  3.1 2.5 %fusion.7 = bf16[1,16,512,64]{2,3,1,0:T(8,128)(2,1)S(1)} fusion(bf16[512,512,1]{1,0,2:T(8,128)(2,1)} %constant.84, bf16[64,64,1]{1,0,2:T(8,128)(2,1)S(1)} %copy-done.2, bf16[16,512,64]{2,1,0:T(8,128)(2,1)S(1)} %reshape.69), kind=kOutput, calls=%fused_computation.18 | convolution fusion | flops 605028352 | bytes 2629632 | tf_op jit(solution)/shard_map/mxqz,yq->mxyz/dot_general | solution.py:60
  5.6 1.1 copy.15
  6.6 1.7 convert_element_type.68
  8.3 1.5 fusion.25
  9.9 7.7 %collective-permute-start = (bf16[1,15,32768]{2,1,0:T(8,128)(2,1)}, bf16[1,15,32768]{2,1,0:T(8,128)(2,1)}, u32[]{:S(2)}, u32[]{:S(2)}) collective-permute-start(bf16[1,15,32768]{2,1,0:T(8,128)(2,1)} %get-tuple-element.11), channel_id=1, source_target_pairs={{0,1},{1,2},{2,3},{3,4},{4,5},{5,6},{6,7},{7,8},{8,9},{9,10},{10,1... | collective-permute-start | bytes 2949128 | tf_op jit(solution)/shard_map/ppermute | solution.py:23
  17.6 0.0 copy-start.3
  17.6 0.0 copy-start.4
  17.6 1.9 collective-permute-start.1
  19.6 2.9 %reshape.68 = bf16[8192,128]{1,0:T(8,128)(2,1)S(1)} reshape(bf16[2,1,16,32768]{3,2,1,0:T(8,128)(2,1)} %param.14) | data formatting | bytes 4194304 | tf_op jit(solution)/shard_map/reshape | solution.py:175
  22.4 0.0 copy-done.3
  22.5 0.0 copy-done.4
  22.5 0.0 copy-start.7
  22.5 14.9 %gather_fusion = bf16[4096,128]{1,0:T(8,128)(2,1)} fusion(bf16[8192,128]{1,0:T(8,128)(2,1)S(1)} %reshape.68, s32[4096]{0:T(1024)S(1)} %get-tuple-element.17), kind=kCustom, calls=%fused_computation | custom fusion | bytes 2113536 | tf_op jit(solution)/shard_map/gather | solution.py:175
  37.4 4.0 %collective-permute-done = bf16[1,15,32768]{2,1,0:T(8,128)(2,1)} collective-permute-done((bf16[1,15,32768]{2,1,0:T(8,128)(2,1)}, bf16[1,15,32768]{2,1,0:T(8,128)(2,1)}, u32[]{:S(2)}, u32[]{:S(2)}) %collective-permute-start) | collective-permute-done | bytes 983072 | tf_op jit(solution)/shard_map/ppermute | solution.py:23
  41.4 22.8 %collective-permute-done.1 = bf16[1,15,32768]{2,1,0:T(8,128)(2,1)} collective-permute-done((bf16[1,15,32768]{2,1,0:T(8,128)(2,1)}, bf16[1,15,32768]{2,1,0:T(8,128)(2,1)}, u32[]{:S(2)}, u32[]{:S(2)}) %collective-permute-start.1) | collective-permute-done | bytes 983072 | tf_op jit(solution)/shard_map/ppermute | solution.py:26
  64.3 3.8 %convolution_bitcast_fusion = f32[1,16,32768]{2,1,0:T(8,128)} fusion(bf16[16,46]{1,0:T(8,128)(2,1)S(1)} %copy-done.7, bf16[1,15,32768]{2,1,0:T(8,128)(2,1)} %collective-permute-done.1, bf16[1,16,32768]{2,1,0:T(8,128)(2,1)S(1)} %convert_element_type.68, bf16[1,15,32768]{2,1,0:T(8,128)(2,1)} %collective-permute-done), kind=kOutput, calls=%fused_computation.1 | convolution fusion | flops 57278464 | bytes 5113280 | tf_op jit(solution)/shard_map/ip,mpc->mic/dot_general | solution.py:66
  68.1 1.7 reshape.71.field_ref
  69.8 5.9 %shard_map.127 = f32[4096,128]{1,0:T(8,128)S(1)} custom-call(s32[4096]{0:T(1024)S(1)} %get-tuple-element.18.index_ref, f32[4096,128]{1,0:T(8,128)S(1)} %reshape.71.field_ref), custom_call_target="tpu_custom_call" | custom-call | tf_op jit(solution)/shard_map/pallas_call | solution.py:91
  75.8 0.0 copy-start.5
  75.8 0.0 copy-start.6
  75.8 0.0 copy-done.1
  75.8 1.6 select_reduce_fusion
  77.4 1.9 collective-permute-start.2
  79.3 1.1 collective-permute-done.2
  80.5 3.5 %collective-permute-start.3 = (f32[4096]{0:T(1024)S(1)}, f32[4096]{0:T(1024)S(1)}, u32[]{:S(2)}, u32[]{:S(2)}) collective-permute-start(f32[4096]{0:T(1024)S(1)} %add.47), channel_id=1, source_target_pairs={{0,64},{32,96},{64,0},{96,32},{128,192},{160,224},{192,128},{224,1... | collective-permute-start | bytes 49160 | tf_op jit(solution)/shard_map/ppermute | solution.py:73
  83.9 2.1 collective-permute-done.3
  86.1 5.1 %collective-permute-start.4 = (f32[4096]{0:T(1024)S(1)}, f32[4096]{0:T(1024)S(1)}, u32[]{:S(2)}, u32[]{:S(2)}) collective-permute-start(f32[4096]{0:T(1024)S(1)} %add.48), channel_id=1, source_target_pairs={{0,128},{32,160},{64,192},{96,224},{128,0},{160,32},{192,64},{224,... | collective-permute-start | bytes 49160 | tf_op jit(solution)/shard_map/ppermute | solution.py:73
  91.2 2.0 collective-permute-done.4
  93.2 1.9 collective-permute-start.5
  95.8 11.8 %collective-permute-done.5 = f32[4096]{0:T(1024)S(1)} collective-permute-done((f32[4096]{0:T(1024)S(1)}, f32[4096]{0:T(1024)S(1)}, u32[]{:S(2)}, u32[]{:S(2)}) %collective-permute-start.5) | collective-permute-done | bytes 16416 | tf_op jit(solution)/shard_map/ppermute | solution.py:73
  107.6 0.0 copy-done.6
  107.6 5.6 %collective-permute-start.6 = (s32[4096]{0:T(1024)S(1)}, s32[4096]{0:T(1024)S(1)}, u32[]{:S(2)}, u32[]{:S(2)}) collective-permute-start(s32[4096]{0:T(1024)S(1)} %copy-done.3), channel_id=1, source_target_pairs={{0,1},{1,2},{2,3},{3,4},{4,5},{5,6},{6,7},{7,8},{8,9},{9,10},{10,1... | collective-permute-start | bytes 49160 | tf_op jit(solution)/shard_map/ppermute | solution.py:156
  113.2 2.9 %collective-permute-start.8 = (f32[4096]{0:T(1024)S(1)}, f32[4096]{0:T(1024)S(1)}, u32[]{:S(2)}, u32[]{:S(2)}) collective-permute-start(f32[4096]{0:T(1024)S(1)} %multiply_multiply_fusion), channel_id=1, source_target_pairs={{0,1},{1,2},{2,3},{3,4},{4,5},{5,6},{6,7},{7,8},{8,9},{9,10},{10,1... | collective-permute-start | bytes 49160 | tf_op jit(solution)/shard_map/ppermute | solution.py:156
  116.1 2.9 %collective-permute-start.9 = (f32[4096]{0:T(1024)S(1)}, f32[4096]{0:T(1024)S(1)}, u32[]{:S(2)}, u32[]{:S(2)}) collective-permute-start(f32[4096]{0:T(1024)S(1)} %multiply_multiply_fusion), channel_id=1, source_target_pairs={{1,0},{2,1},{3,2},{4,3},{5,4},{6,5},{7,6},{8,7},{9,8},{10,9},{11,1... | collective-permute-start | bytes 49160 | tf_op jit(solution)/shard_map/ppermute | solution.py:157
  119.0 2.1 collective-permute-start.7
  121.2 0.0 collective-permute-done.6
  121.2 11.0 %collective-permute-done.7 = s32[4096]{0:T(1024)S(1)} collective-permute-done((s32[4096]{0:T(1024)S(1)}, s32[4096]{0:T(1024)S(1)}, u32[]{:S(2)}, u32[]{:S(2)}) %collective-permute-start.7) | collective-permute-done | bytes 16416 | tf_op jit(solution)/shard_map/ppermute | solution.py:157
  132.2 0.0 collective-permute-done.8
  132.2 0.0 collective-permute-done.9
  132.3 81.5 %shard_map.128 = bf16[11776,128]{1,0:T(8,128)(2,1)S(1)} custom-call(s32[12288]{0:T(1024)S(1)} %fusion.10.index_ref, f32[12288]{0:T(1024)S(1)} %pad_maximum_fusion.value_ref), custom_call_target="tpu_custom_call" | custom-call | tf_op jit(solution)/shard_map/pallas_call | solution.py:136
  213.8 3.2 %reshape.72 = bf16[46,32768]{1,0:T(8,128)(2,1)} reshape(bf16[11776,128]{1,0:T(8,128)(2,1)S(1)} %shard_map.128) | data formatting | bytes 6029312 | tf_op jit(solution)/shard_map/reshape.7
  217.0 2.4 %fusion = bf16[1,16,32768]{2,1,0:T(8,128)(2,1)S(1)} fusion(bf16[46,32768]{1,0:T(8,128)(2,1)} %reshape.72, bf16[16,46]{1,0:T(8,128)(2,1)S(1)} %copy-done.7), kind=kOutput, calls=%fused_computation.3 | convolution fusion | flops 48758784 | bytes 4064704 | tf_op jit(solution)/shard_map/ip,mpc->mic/dot_general | solution.py:66
  219.4 2.3 reshape.73
  221.7 4.9 %fusion.8 = f32[16,512,64]{2,1,0:T(8,128)} fusion(bf16[64,64,1]{1,0,2:T(8,128)(2,1)S(1)} %copy-done.2, bf16[16,512,64]{2,1,0:T(8,128)(2,1)S(1)} %reshape.73, bf16[512,512,1]{1,0,2:T(8,128)(2,1)} %constant.84), kind=kOutput, calls=%fused_computation.19 | convolution fusion | flops 604504064 | bytes 3678208 | tf_op jit(solution)/shard_map/mxyq,zq->mxyz/dot_general | solution.py:52
  226.6 3.0 %reshape.75 = f32[1,16,32768]{2,1,0:T(8,128)S(1)} reshape(f32[16,512,64]{2,1,0:T(8,128)} %fusion.8) | data formatting | bytes 4194304 | tf_op jit(solution)/shard_map/reshape | solution.py:53
  229.6 1.5 convert_add_fusion
  (17 shorter events, 0.1 us)
Async XLA Ops:
  0.0 3.1 %copy-start.2 = (bf16[64,64,1]{1,0,2:T(8,128)(2,1)S(1)}, bf16[64,64,1]{1,0,2:T(8,128)(2,1)}, u32[]{:S(2)}) copy-start(bf16[64,64,1]{1,0,2:T(8,128)(2,1)} %constant.83) | copy-start | bytes 24580
  9.9 31.6 %collective-permute-start = (bf16[1,15,32768]{2,1,0:T(8,128)(2,1)}, bf16[1,15,32768]{2,1,0:T(8,128)(2,1)}, u32[]{:S(2)}, u32[]{:S(2)}) collective-permute-start(bf16[1,15,32768]{2,1,0:T(8,128)(2,1)} %get-tuple-element.11), channel_id=1, source_target_pairs={{0,1},{1,2},{2,3},{3,4},{4,5},{5,6},{6,7},{7,8},{8,9},{9,10},{10,1... | collective-permute-start | bytes 2949128 | tf_op jit(solution)/shard_map/ppermute | solution.py:23
  17.6 4.8 %copy-start.3 = (s32[4096]{0:T(1024)S(1)}, s32[4096]{0:T(1024)}, u32[]{:S(2)}) copy-start(s32[4096]{0:T(1024)} %param.15) | copy-start | bytes 49156
  17.6 4.8 %copy-start.4 = (s32[4096]{0:T(1024)S(1)}, s32[4096]{0:T(1024)}, u32[]{:S(2)}) copy-start(s32[4096]{0:T(1024)} %param.16) | copy-start | bytes 49156
  17.6 46.6 %collective-permute-start.1 = (bf16[1,15,32768]{2,1,0:T(8,128)(2,1)}, bf16[1,15,32768]{2,1,0:T(8,128)(2,1)}, u32[]{:S(2)}, u32[]{:S(2)}) collective-permute-start(bf16[1,15,32768]{2,1,0:T(8,128)(2,1)} %get-tuple-element.12), channel_id=1, source_target_pairs={{1,0},{2,1},{3,2},{4,3},{5,4},{6,5},{7,6},{8,7},{9,8},{10,9},{11,1... | collective-permute-start | bytes 2949128 | tf_op jit(solution)/shard_map/ppermute | solution.py:26
  22.5 41.8 %copy-start.7 = (bf16[16,46]{1,0:T(8,128)(2,1)S(1)}, bf16[16,46]{1,0:T(8,128)(2,1)}, u32[]{:S(2)}) copy-start(bf16[16,46]{1,0:T(8,128)(2,1)} %constant.79.clone) | copy-start | bytes 4420
  69.8 6.0 %copy-start.1 = (bf16[4096,128]{1,0:T(8,128)(2,1)S(1)}, bf16[4096,128]{1,0:T(8,128)(2,1)}, u32[]{:S(2)}) copy-start(bf16[4096,128]{1,0:T(8,128)(2,1)} %gather_fusion) | copy-start | bytes 3145732
  75.8 31.8 %copy-start.5 = (f32[4096]{0:T(1024)S(1)}, f32[4096]{0:T(1024)}, u32[]{:S(2)}) copy-start(f32[4096]{0:T(1024)} %param.17) | copy-start | bytes 49156
  75.8 31.8 %copy-start.6 = (f32[4096]{0:T(1024)S(1)}, f32[4096]{0:T(1024)}, u32[]{:S(2)}) copy-start(f32[4096]{0:T(1024)} %param.18) | copy-start | bytes 49156
  77.4 3.1 %collective-permute-start.2 = (f32[4096]{0:T(1024)S(1)}, f32[4096]{0:T(1024)S(1)}, u32[]{:S(2)}, u32[]{:S(2)}) collective-permute-start(f32[4096]{0:T(1024)S(1)} %mul.27), channel_id=1, source_target_pairs={{0,32},{32,0},{64,96},{96,64},{128,160},{160,128},{192,224},{224,1... | collective-permute-start | bytes 49160 | tf_op jit(solution)/shard_map/ppermute | solution.py:73
  80.5 5.6 %collective-permute-start.3 = (f32[4096]{0:T(1024)S(1)}, f32[4096]{0:T(1024)S(1)}, u32[]{:S(2)}, u32[]{:S(2)}) collective-permute-start(f32[4096]{0:T(1024)S(1)} %add.47), channel_id=1, source_target_pairs={{0,64},{32,96},{64,0},{96,32},{128,192},{160,224},{192,128},{224,1... | collective-permute-start | bytes 49160 | tf_op jit(solution)/shard_map/ppermute | solution.py:73
  86.1 7.1 %collective-permute-start.4 = (f32[4096]{0:T(1024)S(1)}, f32[4096]{0:T(1024)S(1)}, u32[]{:S(2)}, u32[]{:S(2)}) collective-permute-start(f32[4096]{0:T(1024)S(1)} %add.48), channel_id=1, source_target_pairs={{0,128},{32,160},{64,192},{96,224},{128,0},{160,32},{192,64},{224,... | collective-permute-start | bytes 49160 | tf_op jit(solution)/shard_map/ppermute | solution.py:73
  93.2 14.3 %collective-permute-start.5 = (f32[4096]{0:T(1024)S(1)}, f32[4096]{0:T(1024)S(1)}, u32[]{:S(2)}, u32[]{:S(2)}) collective-permute-start(f32[4096]{0:T(1024)S(1)} %add.49), channel_id=1, source_target_pairs={{0,256},{32,288},{64,320},{96,352},{128,384},{160,416},{192,448},{... | collective-permute-start | bytes 49160 | tf_op jit(solution)/shard_map/ppermute | solution.py:73
  107.6 13.6 %collective-permute-start.6 = (s32[4096]{0:T(1024)S(1)}, s32[4096]{0:T(1024)S(1)}, u32[]{:S(2)}, u32[]{:S(2)}) collective-permute-start(s32[4096]{0:T(1024)S(1)} %copy-done.3), channel_id=1, source_target_pairs={{0,1},{1,2},{2,3},{3,4},{4,5},{5,6},{6,7},{7,8},{8,9},{9,10},{10,1... | collective-permute-start | bytes 49160 | tf_op jit(solution)/shard_map/ppermute | solution.py:156
  113.2 19.1 %collective-permute-start.8 = (f32[4096]{0:T(1024)S(1)}, f32[4096]{0:T(1024)S(1)}, u32[]{:S(2)}, u32[]{:S(2)}) collective-permute-start(f32[4096]{0:T(1024)S(1)} %multiply_multiply_fusion), channel_id=1, source_target_pairs={{0,1},{1,2},{2,3},{3,4},{4,5},{5,6},{6,7},{7,8},{8,9},{9,10},{10,1... | collective-permute-start | bytes 49160 | tf_op jit(solution)/shard_map/ppermute | solution.py:156
  116.1 16.1 %collective-permute-start.9 = (f32[4096]{0:T(1024)S(1)}, f32[4096]{0:T(1024)S(1)}, u32[]{:S(2)}, u32[]{:S(2)}) collective-permute-start(f32[4096]{0:T(1024)S(1)} %multiply_multiply_fusion), channel_id=1, source_target_pairs={{1,0},{2,1},{3,2},{4,3},{5,4},{6,5},{7,6},{8,7},{9,8},{10,9},{11,1... | collective-permute-start | bytes 49160 | tf_op jit(solution)/shard_map/ppermute | solution.py:157
  119.0 13.1 %collective-permute-start.7 = (s32[4096]{0:T(1024)S(1)}, s32[4096]{0:T(1024)S(1)}, u32[]{:S(2)}, u32[]{:S(2)}) collective-permute-start(s32[4096]{0:T(1024)S(1)} %copy-done.3), channel_id=1, source_target_pairs={{1,0},{2,1},{3,2},{4,3},{5,4},{6,5},{7,6},{8,7},{9,8},{10,9},{11,1... | collective-permute-start | bytes 49160 | tf_op jit(solution)/shard_map/ppermute | solution.py:157
  226.6 3.0 %copy-start = (bf16[1,16,32768]{2,1,0:T(8,128)(2,1)S(1)}, bf16[1,16,32768]{2,1,0:T(8,128)(2,1)}, u32[]{:S(2)}) copy-start(bf16[1,16,32768]{2,1,0:T(8,128)(2,1)} %param.13) | copy-start | bytes 3145732
